TPU v7x, 32 devices: a whole 2x2x4 slice. The times are simulated.
32 devices in a mesh: dp: 4 (over y, core), tile: 8 (over z, x).
Axes of the slice: x: 2, y: 2, z: 4, core: 2. Of those that a mesh axis runs over, the one named last changes fastest.
Arguments:
- queries: bfloat16 [4, 8, 1024, 1664], P('dp', 'tile'), may hold values from -48 to 48
- keys: bfloat16 [4, 8, 1024, 1664], P('dp', 'tile'), may hold values from -48 to 48
- values: bfloat16 [4, 8, 1024, 1664], P('dp', 'tile'), may hold values from -6 to 6
- page_info: int32 [4, 5], replicated, may hold values from 0 to 256, as said below
Outputs:
- llm_rows: bfloat16 [9216, 6656], P(('dp', 'tile'))
Inputs may be any that keep to these rules, and one draw needn't show every extreme that they name: `page_info`: columns are 1 to 4, columns times rows is at most 7, tiles fill slots from the first tile slot on within the page, the thumbnail slot lies outside them, text rows at most 256; some page has 7 tiles starting at slot 0, some page 8 - 1 tiles ending at slot 7, and some page 256 text rows.
All inputs are finite; a program needn't handle non-finite values.
Results may differ from a plain program's by a relative error of at most 0.0047.
Values may be sent and summed in bfloat16 or wider, within the bound.
No kernel may reach another device: no remote copies, remote signals or barrier semaphores. Data moves between devices by JAX's collectives and lax.ppermute only.
A program may use at most 256 MiB of HBM per device.

v0:
```python
import jax
import jax.numpy as jnp
from jax import lax
from jax.experimental import pallas as pl
from jax.experimental.pallas import tpu as pltpu
from jax.sharding import PartitionSpec as P

HEADS = 13
HD = 128
GRID = 32
TXTMAX = 256
HH = 1664
TOK = 1024
SHUF = 256
HEAD_CHUNKS = ((0, 4), (4, 8), (8, 11), (11, 13))


def passed_along(value, axis, steps):
    count = lax.axis_size(axis)
    initial, last = (max(0, -steps), min(count, count - steps))
    return lax.ppermute(value, axis, [(source, source + steps) for source in range(initial, last)])


def block_terms(query, k_ref, v_ref):
    scores = lax.dot_general(
        query, k_ref[...], (((1,), (1,)), ((), ())), preferred_element_type=jnp.float32
    ) * HD ** (-0.5)
    largest = jnp.max(scores, axis=1, keepdims=True)
    weights = jnp.exp(scores - largest).astype(jnp.bfloat16)
    ones = jnp.ones((TOK, HD), jnp.bfloat16)
    both = jnp.dot(
        weights, jnp.concatenate([v_ref[...], ones], axis=1), preferred_element_type=jnp.float32
    )
    return both[:, :HD], largest, both[:, HD : HD + 1]


def merge_block(flag, query, k_ref, v_ref, acc_ref, top_ref, sum_ref):
    @pl.when(flag != 0)
    def _():
        numerator, largest, totals = block_terms(query, k_ref, v_ref)
        old_top = top_ref[...]
        new_top = jnp.maximum(old_top, largest)
        keep = jnp.exp(old_top - new_top)
        take = jnp.exp(largest - new_top)
        acc_ref[...] = acc_ref[...] * keep + numerator * take
        sum_ref[...] = sum_ref[...] * keep + totals * take
        top_ref[...] = new_top


def near_kernel(flags_ref, q_ref, k0, v0, k1, v1, k2, v2, acc_prev, top_prev, sum_prev, acc_ref, top_ref, sum_ref):
    query = q_ref[...]
    numerator, largest, totals = block_terms(query, k0, v0)
    acc_ref[...] = numerator
    top_ref[0] = largest
    sum_ref[0] = totals
    merge_block(flags_ref[0], query, k1, v1, acc_ref, top_ref.at[0], sum_ref.at[0])
    merge_block(flags_ref[1], query, k2, v2, acc_ref, top_ref.at[0], sum_ref.at[0])


def thumb_kernel(flags_ref, q_ref, k3, v3, acc_in, top_in, sum_in, o_ref, acc_ref, top_ref, sum_ref):
    acc_ref[...] = acc_in[...]
    top_ref[...] = top_in[0]
    sum_ref[...] = sum_in[0]
    merge_block(flags_ref[2], q_ref[...], k3, v3, acc_ref, top_ref, sum_ref)
    o_ref[...] = (acc_ref[...] / sum_ref[...]).astype(o_ref.dtype)


def attend_near(flags, query_cols, blocks, first_head, head_count, state):
    q_spec = pl.BlockSpec((TOK, HD), lambda h, flags: (0, h))
    v_spec = pl.BlockSpec((TOK, HD), lambda h, flags: (0, head_count + h))
    acc_spec = pl.BlockSpec((TOK, HD), lambda h, flags: (0, first_head + h))
    stat_spec = pl.BlockSpec((1, TOK, 1), lambda h, flags: (first_head + h, 0, 0))
    held = pl.BlockSpec(memory_space=pl.ANY)
    operands = []
    for both in blocks:
        operands += [both, both]
    count = 1 + len(operands)
    return pl.pallas_call(
        near_kernel,
        grid_spec=pltpu.PrefetchScalarGridSpec(
            num_scalar_prefetch=1,
            grid=(head_count,),
            in_specs=[q_spec] + [q_spec, v_spec] * len(blocks) + [held] * 3,
            out_specs=[acc_spec, stat_spec, stat_spec],
        ),
        out_shape=[
            jax.ShapeDtypeStruct((TOK, HH), jnp.float32),
            jax.ShapeDtypeStruct((HEADS, TOK, 1), jnp.float32),
            jax.ShapeDtypeStruct((HEADS, TOK, 1), jnp.float32),
        ],
        input_output_aliases={count + 1: 0, count + 2: 1, count + 3: 2},
    )(flags, query_cols, *operands, *state)


def attend_thumb(flags, query_tile, thumb_keys, thumb_values, acc, top, totals):
    q_spec = pl.BlockSpec((TOK, HD), lambda h, flags: (0, h))
    stat_spec = pl.BlockSpec((1, TOK, 1), lambda h, flags: (h, 0, 0))
    return pl.pallas_call(
        thumb_kernel,
        grid_spec=pltpu.PrefetchScalarGridSpec(
            num_scalar_prefetch=1,
            grid=(HEADS,),
            in_specs=[q_spec, q_spec, q_spec, q_spec, stat_spec, stat_spec],
            out_specs=q_spec,
            scratch_shapes=[
                pltpu.VMEM((TOK, HD), jnp.float32),
                pltpu.VMEM((TOK, 1), jnp.float32),
                pltpu.VMEM((TOK, 1), jnp.float32),
            ],
        ),
        out_shape=jax.ShapeDtypeStruct((TOK, HH), jnp.bfloat16),
    )(flags, query_tile, thumb_keys, thumb_values, acc, top, totals)


def pixel_shuffle(attended):
    half_grid = GRID // 2
    width = attended.shape[-1]
    return (
        attended.reshape(half_grid, 2, half_grid, 2, width)
        .transpose(0, 2, 1, 3, 4)
        .reshape(half_grid * half_grid, 4 * width)
    )


def page_layout(page_info):
    columns = page_info[:, 0]
    tile_totals = columns * page_info[:, 1]
    thumbs = page_info[:, 2]
    texts = page_info[:, 3]
    firsts = page_info[:, 4]
    lengths = texts + (tile_totals + 1) * SHUF
    starts = jnp.cumsum(lengths) - lengths
    return (columns, tile_totals, thumbs, texts, starts, firsts)


def body(queries, keys, values, page_info):
    query_tile = queries.reshape(TOK, HH)
    key_tile = keys.reshape(TOK, HH)
    value_tile = values.reshape(TOK, HH)
    slot_count = lax.axis_size("tile")
    page_count = lax.axis_size("dp")
    device_count = page_count * slot_count
    page_index = lax.axis_index("dp")
    slot_index = lax.axis_index("tile")
    columns, tile_totals, thumbs, texts, starts, firsts = page_layout(page_info)
    grid_width = columns[page_index]
    tile_total = tile_totals[page_index]
    thumb_slot = thumbs[page_index]
    grid_pos = slot_index - firsts[page_index]
    is_tile = (grid_pos >= 0) & (grid_pos < tile_total)
    has_left = is_tile & (grid_pos % grid_width > 0)
    has_right = is_tile & (grid_pos % grid_width < grid_width - 1)
    flags = jnp.stack([has_left, has_right, is_tile]).astype(jnp.int32)
    is_thumb = slot_index == thumb_slot
    is_live = is_tile | is_thumb
    row_start = (
        starts[page_index] + texts[page_index] + jnp.where(is_thumb, tile_total, grid_pos) * SHUF
    )
    per_peer = SHUF // device_count
    query_tile = (
        jnp.roll(
            pixel_shuffle(query_tile).reshape(per_peer, device_count, 4 * HH),
            row_start % device_count,
            axis=1,
        )
        .transpose(1, 0, 2)
        .reshape(TOK, HH)
    )

    mine = slot_index == thumb_slot
    thumb_keys = lax.psum(jnp.where(mine, key_tile, jnp.zeros_like(key_tile)), "tile")
    thumb_values = lax.psum(jnp.where(mine, value_tile, jnp.zeros_like(value_tile)), "tile")
    state = (
        jnp.zeros((TOK, HH), jnp.float32),
        jnp.zeros((HEADS, TOK, 1), jnp.float32),
        jnp.zeros((HEADS, TOK, 1), jnp.float32),
    )
    arrived_last = None
    state_before = None
    for first_head, end_head in HEAD_CHUNKS:
        head_count = end_head - first_head
        cols = slice(first_head * HD, end_head * HD)
        own = jnp.concatenate([key_tile[:, cols], value_tile[:, cols]], axis=1)
        if arrived_last is not None:
            arrived_last, state_before, own = lax.optimization_barrier((arrived_last, state_before, own))
        left = passed_along(own, "tile", 1)
        right = passed_along(own, "tile", -1)
        arrived_last = (left, right)
        state_before = state
        state = attend_near(
            flags, query_tile[:, cols], (own, left, right), first_head, head_count, state
        )
    attended = attend_thumb(flags, query_tile, thumb_keys, thumb_values, *state)
    arranged = attended.reshape(device_count, per_peer, 4 * HH)
    arrived = lax.all_to_all(arranged, ("dp", "tile"), split_axis=0, concat_axis=0, tiled=True)
    own_rank = page_index * slot_count + slot_index
    sources = jnp.arange(device_count, dtype=jnp.int32)
    source_page = sources // slot_count
    source_slot = sources % slot_count
    source_grid = source_slot - firsts[source_page]
    source_thumb = source_slot == thumbs[source_page]
    source_live = (source_grid >= 0) & (source_grid < tile_totals[source_page]) | source_thumb
    source_start = (
        starts[source_page]
        + texts[source_page]
        + jnp.where(source_thumb, tile_totals[source_page], source_grid) * SHUF
    )
    first_row = (source_start + (own_rank - source_start) % device_count) // device_count
    shard_rows = SHUF + TXTMAX // slot_count
    targets = first_row[:, None] + jnp.arange(per_peer, dtype=jnp.int32)[None, :]
    targets = jnp.where(source_live[:, None], targets, shard_rows)
    placed = jnp.zeros((shard_rows, 4 * HH), jnp.bfloat16)
    return placed.at[targets.reshape(-1)].set(arrived.reshape(-1, 4 * HH), mode="drop")


def solution(mesh):
    placed = (
        P("dp", "tile", None, None),
        P("dp", "tile", None, None),
        P("dp", "tile", None, None),
        P(),
    )
    return jax.shard_map(
        body, mesh=mesh, in_specs=placed, out_specs=P(("dp", "tile"), None), check_vma=False
    )
```

profile of v0, /device:TPU:0, one launch (start us, length us, event | category | flops | bytes accessed | tf_op | source)
XLA Modules:
  0.0 558.5 jit_solution(16609706016902835582)
XLA Ops:
  10.3 6.2 %collective-permute-start = (bf16[1024,1024]{1,0:T(8,128)(2,1)S(1)}, bf16[1024,1024]{1,0:T(8,128)(2,1)}, u32[]{:S(2)}, u32[]{:S(2)}) collective-permute-start(bf16[1024,1024]{1,0:T(8,128)(2,1)S(1)} %pad_maximum_fusion.k0.v0), channel_id=1, source_target_pairs={{0,1},{1,2},{2,3},{3,4},{4,5},{5,6},{6,7},{8,9},{9,10},{10,11},{11... | collective-permute-start | bytes 6291464 | tf_op jit(solution)/shard_map/ppermute | solution.py:21
  28.2 101.1 %collective-permute-done.k1.v1 = bf16[1024,1024]{1,0:T(8,128)(2,1)} collective-permute-done((bf16[1024,1024]{1,0:T(8,128)(2,1)S(1)}, bf16[1024,1024]{1,0:T(8,128)(2,1)}, u32[]{:S(2)}, u32[]{:S(2)}) %collective-permute-start) | collective-permute-done | bytes 2097184 | tf_op jit(solution)/shard_map/ppermute | solution.py:21
  129.3 5.9 %collective-permute-start.2 = (bf16[1024,1024]{1,0:T(8,128)(2,1)}, bf16[1024,1024]{1,0:T(8,128)(2,1)}, u32[]{:S(2)}, u32[]{:S(2)}) collective-permute-start(bf16[1024,1024]{1,0:T(8,128)(2,1)} %pad_maximum_fusion.1.k0.v0), channel_id=1, source_target_pairs={{0,1},{1,2},{2,3},{3,4},{4,5},{5,6},{6,7},{8,9},{9,10},{10,11},{11... | collective-permute-start | bytes 6291464 | tf_op jit(solution)/shard_map/ppermute | solution.py:21
  146.9 6.6 %reshape_reshape.6 = bf16[16,2,16,2,1664]{4,3,2,1,0:T(2,128)(2,1)S(1)} reshape(bf16[1,1,1024,1664]{3,2,1,0:T(8,128)(2,1)} %param.4) | data formatting | bytes 6815744 | tf_op jit(solution)/shard_map/reshape;reshape | solution.py:119
  153.5 4.3 copy.20
  157.8 7.3 %reshape_reshape.7 = bf16[8,32,6656]{2,1,0:T(8,128)(2,1)S(1)} reshape(bf16[16,16,2,2,1664]{4,3,2,1,0:T(2,128)(2,1)} %bitcast.68) | data formatting | bytes 6815744 | tf_op jit(solution)/shard_map/reshape;reshape | solution.py:162
  170.9 5.4 reshape.198.q_ref
  192.3 13.5 %shard_map.46 = (f32[1024,1664]{1,0:T(8,128)}, f32[13,1024,1]{2,1,0:T(8,128)}, f32[13,1024,1]{2,1,0:T(8,128)}) custom-call(s32[3]{0:T(128)} %add_convert_fusion.flags_ref, bf16[1024,512]{1,0:T(8,128)(2,1)} %get-tuple-element.44.q_ref, bf16[1024,1024]{1,0:T(8,128)(2,1)} %copy-done.1, ...), custom_call_target="tpu_custom_call", output_to_operand_aliasing={{0}: (8, {}), {1}: (9, {}), {2}: (10, {})} | custom-call | tf_op jit(solution)/shard_map/pallas_call | solution.py:78
  205.8 34.3 %collective-permute-done.2.k1.v1 = bf16[1024,1024]{1,0:T(8,128)(2,1)} collective-permute-done((bf16[1024,1024]{1,0:T(8,128)(2,1)}, bf16[1024,1024]{1,0:T(8,128)(2,1)}, u32[]{:S(2)}, u32[]{:S(2)}) %collective-permute-start.2) | collective-permute-done | bytes 2097184 | tf_op jit(solution)/shard_map/ppermute | solution.py:21
  240.1 5.6 %collective-permute-start.4 = (bf16[1024,768]{1,0:T(8,128)(2,1)}, bf16[1024,768]{1,0:T(8,128)(2,1)}, u32[]{:S(2)}, u32[]{:S(2)}) collective-permute-start(bf16[1024,768]{1,0:T(8,128)(2,1)} %pad_maximum_fusion.2.k0.v0), channel_id=1, source_target_pairs={{0,1},{1,2},{2,3},{3,4},{4,5},{5,6},{6,7},{8,9},{9,10},{10,11},{11... | collective-permute-start | bytes 4718600 | tf_op jit(solution)/shard_map/ppermute | solution.py:21
  250.2 13.7 %shard_map.47 = (f32[1024,1664]{1,0:T(8,128)}, f32[13,1024,1]{2,1,0:T(8,128)}, f32[13,1024,1]{2,1,0:T(8,128)}) custom-call(s32[3]{0:T(128)} %add_convert_fusion.flags_ref, bf16[1024,512]{1,0:T(8,128)(2,1)} %get-tuple-element.43.q_ref, bf16[1024,1024]{1,0:T(8,128)(2,1)} %pad_maximum_fusion.1.k0.v0, ...), custom_call_target="tpu_custom_call", output_to_operand_aliasing={{0}: (8, {}), {1}: (9, {}), {2}: (10, {})} | custom-call | tf_op jit(solution)/shard_map/pallas_call | solution.py:78
  263.8 63.5 %collective-permute-done.4.k1.v1 = bf16[1024,768]{1,0:T(8,128)(2,1)} collective-permute-done((bf16[1024,768]{1,0:T(8,128)(2,1)}, bf16[1024,768]{1,0:T(8,128)(2,1)}, u32[]{:S(2)}, u32[]{:S(2)}) %collective-permute-start.4) | collective-permute-done | bytes 1572896 | tf_op jit(solution)/shard_map/ppermute | solution.py:21
  327.4 5.4 collective-permute-start.6
  335.8 10.9 %shard_map.48 = (f32[1024,1664]{1,0:T(8,128)}, f32[13,1024,1]{2,1,0:T(8,128)}, f32[13,1024,1]{2,1,0:T(8,128)}) custom-call(s32[3]{0:T(128)} %add_convert_fusion.flags_ref, bf16[1024,384]{1,0:T(8,128)(2,1)} %slice.143.q_ref, bf16[1024,768]{1,0:T(8,128)(2,1)} %pad_maximum_fusion.2.k0.v0, ...), custom_call_target="tpu_custom_call", output_to_operand_aliasing={{0}: (8, {}), {1}: (9, {}), {2}: (10, {})} | custom-call | tf_op jit(solution)/shard_map/pallas_call | solution.py:78
  346.7 28.5 %collective-permute-done.6.k1.v1 = bf16[1024,512]{1,0:T(8,128)(2,1)} collective-permute-done((bf16[1024,512]{1,0:T(8,128)(2,1)}, bf16[1024,512]{1,0:T(8,128)(2,1)}, u32[]{:S(2)}, u32[]{:S(2)}) %collective-permute-start.6) | collective-permute-done | bytes 1048608 | tf_op jit(solution)/shard_map/ppermute | solution.py:21
  375.3 8.5 %shard_map.49 = (f32[1024,1664]{1,0:T(8,128)}, f32[13,1024,1]{2,1,0:T(8,128)}, f32[13,1024,1]{2,1,0:T(8,128)}) custom-call(s32[3]{0:T(128)} %add_convert_fusion.flags_ref, bf16[1024,256]{1,0:T(8,128)(2,1)} %slice.132.q_ref, bf16[1024,512]{1,0:T(8,128)(2,1)} %pad_maximum_fusion.3.k0.v0, ...), custom_call_target="tpu_custom_call", output_to_operand_aliasing={{0}: (8, {}), {1}: (9, {}), {2}: (10, {})} | custom-call | tf_op jit(solution)/shard_map/pallas_call | solution.py:78
  383.8 4.6 all-reduce.3.cloned.1.call-done
  388.4 17.0 %shard_map.50 = bf16[1024,1664]{1,0:T(8,128)(2,1)} custom-call(s32[3]{0:T(128)} %add_convert_fusion.flags_ref, bf16[1024,1664]{1,0:T(8,128)(2,1)} %copy-done, bf16[1024,1664]{1,0:T(8,128)(2,1)} %get-tuple-element.35.k3, bf16[1024,1664]{1,0:T(8,128)(2,1)} %get-tuple-element.36.v3, f32[1024,1664]{1,0:T(8,128)} %get-tuple-element.32.acc_in, ...), custom_call_target="tpu_custom_call" | custom-call | tf_op jit(solution)/shard_map/pallas_call | solution.py:98
  405.4 6.7 %reshape.201 = bf16[32,8,6656]{2,1,0:T(8,128)(2,1)} reshape(bf16[1024,1664]{1,0:T(8,128)(2,1)} %shard_map.50) | data formatting | bytes 6815744 | tf_op jit(solution)/shard_map/reshape | solution.py:194
  412.0 53.5 %all-to-all-start = ((bf16[32,8,6656]{2,1,0:T(8,128)(2,1)}), bf16[32,8,6656]{2,1,0:T(8,128)(2,1)S(1)}, u32[]{:S(2)}, u32[]{:S(2)}) async-start(bf16[32,8,6656]{2,1,0:T(8,128)(2,1)} %reshape.201), calls=%async_computation | async-start | bytes 6815744 | tf_op jit(solution)/shard_map/all_to_all | solution.py:195
  466.3 7.7 %and_or_fusion = (pred[32]{0:T(512)(128)(4,1)S(1)}, s32[32,1]{0,1:T(1,128)S(1)}, s32[32]{0:T(128)S(1)}, pred[32]{0:T(512)(128)(4,1)S(1)}) fusion(s32[]{:T(128)} %bitcast.8, s32[]{:T(128)} %bitcast.7, s32[]{:T(128)} %bitcast.6, s32[]{:T(128)} %bitcast.5, s32[]{:T(128)} %bitcast.3, s32[]{:T(128)} %bitcast.2, s32[]{:T(128)} %bitcast.1, s32[]{:T(128)} %bitcast, ...), kind=kLoop, calls=%fused_computation.31 | loop fusion | flops 1120 | bytes 368 | tf_op jit(solution)/shard_map/or | solution.py:202
  474.0 5.0 and_select_fusion
  479.2 64.6 %all-to-all-done = bf16[32,8,6656]{2,1,0:T(8,128)(2,1)S(1)} async-done(((bf16[32,8,6656]{2,1,0:T(8,128)(2,1)}), bf16[32,8,6656]{2,1,0:T(8,128)(2,1)S(1)}, u32[]{:S(2)}, u32[]{:S(2)}) %all-to-all-start) | async-done | bytes 3407904 | tf_op jit(solution)/shard_map/all_to_all | solution.py:195
  543.8 7.4 %scatter_custom_fusion = bf16[288,6656]{1,0:T(8,128)(2,1)} fusion(s32[256]{0:T(256)S(1)} %bitcast.69, bf16[32,8,6656]{2,1,0:T(8,128)(2,1)S(1)} %all-to-all-done, bf16[]{:T(256)} %constant.98.clone.1), kind=kCustom, calls=%fused_computation.5 | custom fusion | bytes 7241730 | tf_op jit(solution)/shard_map/scatter | solution.py:213
  (49 shorter events, 52.3 us)
Async XLA Ops:
  6.5 381.8 %all-reduce.3.cloned.1.call-start = ((), (), s32[]{:S(2)}) async-start(), calls=%async_computation.1 | async-start | bytes 13631488 | tf_op jit(solution)/shard_map/psum | solution.py:171
  10.0 7.8 %copy-start.3 = (s32[4,5]{1,0:T(4,128)S(1)}, s32[4,5]{1,0:T(4,128)}, u32[]{:S(2)}) copy-start(s32[4,5]{1,0:T(4,128)} %param.7) | copy-start | bytes 244
  10.3 12.9 %copy-start.1 = (bf16[1024,1024]{1,0:T(8,128)(2,1)}, bf16[1024,1024]{1,0:T(8,128)(2,1)S(1)}, u32[]{:S(2)}) copy-start(bf16[1024,1024]{1,0:T(8,128)(2,1)S(1)} %pad_maximum_fusion.k0.v0) | copy-start | bytes 6291460
  10.3 119.0 %collective-permute-start = (bf16[1024,1024]{1,0:T(8,128)(2,1)S(1)}, bf16[1024,1024]{1,0:T(8,128)(2,1)}, u32[]{:S(2)}, u32[]{:S(2)}) collective-permute-start(bf16[1024,1024]{1,0:T(8,128)(2,1)S(1)} %pad_maximum_fusion.k0.v0), channel_id=1, source_target_pairs={{0,1},{1,2},{2,3},{3,4},{4,5},{5,6},{6,7},{8,9},{9,10},{10,11},{11... | collective-permute-start | bytes 6291464 | tf_op jit(solution)/shard_map/ppermute | solution.py:21
  16.5 112.8 %collective-permute-start.1 = (bf16[1024,1024]{1,0:T(8,128)(2,1)S(1)}, bf16[1024,1024]{1,0:T(8,128)(2,1)}, u32[]{:S(2)}, u32[]{:S(2)}) collective-permute-start(bf16[1024,1024]{1,0:T(8,128)(2,1)S(1)} %pad_maximum_fusion.k0.v0), channel_id=1, source_target_pairs={{1,0},{2,1},{3,2},{4,3},{5,4},{6,5},{7,6},{9,8},{10,9},{11,10},{12... | collective-permute-start | bytes 6291464 | tf_op jit(solution)/shard_map/ppermute | solution.py:21
  19.1 4.1 copy-start.2
  129.3 110.8 %collective-permute-start.2 = (bf16[1024,1024]{1,0:T(8,128)(2,1)}, bf16[1024,1024]{1,0:T(8,128)(2,1)}, u32[]{:S(2)}, u32[]{:S(2)}) collective-permute-start(bf16[1024,1024]{1,0:T(8,128)(2,1)} %pad_maximum_fusion.1.k0.v0), channel_id=1, source_target_pairs={{0,1},{1,2},{2,3},{3,4},{4,5},{5,6},{6,7},{8,9},{9,10},{10,11},{11... | collective-permute-start | bytes 6291464 | tf_op jit(solution)/shard_map/ppermute | solution.py:21
  135.1 104.9 %collective-permute-start.3 = (bf16[1024,1024]{1,0:T(8,128)(2,1)}, bf16[1024,1024]{1,0:T(8,128)(2,1)}, u32[]{:S(2)}, u32[]{:S(2)}) collective-permute-start(bf16[1024,1024]{1,0:T(8,128)(2,1)} %pad_maximum_fusion.1.k0.v0), channel_id=1, source_target_pairs={{1,0},{2,1},{3,2},{4,3},{5,4},{6,5},{7,6},{9,8},{10,9},{11,10},{12... | collective-permute-start | bytes 6291464 | tf_op jit(solution)/shard_map/ppermute | solution.py:21
  176.3 158.7 %copy-start = (bf16[1024,1664]{1,0:T(8,128)(2,1)}, bf16[1024,1664]{1,0:T(8,128)(2,1)S(1)}, u32[]{:S(2)}) copy-start(bf16[1024,1664]{1,0:T(8,128)(2,1)S(1)} %reshape.198.q_ref) | copy-start | bytes 10223620
  240.1 87.3 %collective-permute-start.4 = (bf16[1024,768]{1,0:T(8,128)(2,1)}, bf16[1024,768]{1,0:T(8,128)(2,1)}, u32[]{:S(2)}, u32[]{:S(2)}) collective-permute-start(bf16[1024,768]{1,0:T(8,128)(2,1)} %pad_maximum_fusion.2.k0.v0), channel_id=1, source_target_pairs={{0,1},{1,2},{2,3},{3,4},{4,5},{5,6},{6,7},{8,9},{9,10},{10,11},{11... | collective-permute-start | bytes 4718600 | tf_op jit(solution)/shard_map/ppermute | solution.py:21
  245.7 81.7 %collective-permute-start.5 = (bf16[1024,768]{1,0:T(8,128)(2,1)}, bf16[1024,768]{1,0:T(8,128)(2,1)}, u32[]{:S(2)}, u32[]{:S(2)}) collective-permute-start(bf16[1024,768]{1,0:T(8,128)(2,1)} %pad_maximum_fusion.2.k0.v0), channel_id=1, source_target_pairs={{1,0},{2,1},{3,2},{4,3},{5,4},{6,5},{7,6},{9,8},{10,9},{11,10},{12... | collective-permute-start | bytes 4718600 | tf_op jit(solution)/shard_map/ppermute | solution.py:21
  327.4 47.9 %collective-permute-start.6 = (bf16[1024,512]{1,0:T(8,128)(2,1)}, bf16[1024,512]{1,0:T(8,128)(2,1)}, u32[]{:S(2)}, u32[]{:S(2)}) collective-permute-start(bf16[1024,512]{1,0:T(8,128)(2,1)} %pad_maximum_fusion.3.k0.v0), channel_id=1, source_target_pairs={{0,1},{1,2},{2,3},{3,4},{4,5},{5,6},{6,7},{8,9},{9,10},{10,11},{11... | collective-permute-start | bytes 3145736 | tf_op jit(solution)/shard_map/ppermute | solution.py:21
  332.8 42.5 %collective-permute-start.7 = (bf16[1024,512]{1,0:T(8,128)(2,1)}, bf16[1024,512]{1,0:T(8,128)(2,1)}, u32[]{:S(2)}, u32[]{:S(2)}) collective-permute-start(bf16[1024,512]{1,0:T(8,128)(2,1)} %pad_maximum_fusion.3.k0.v0), channel_id=1, source_target_pairs={{1,0},{2,1},{3,2},{4,3},{5,4},{6,5},{7,6},{9,8},{10,9},{11,10},{12... | collective-permute-start | bytes 3145736 | tf_op jit(solution)/shard_map/ppermute | solution.py:21
  412.0 131.8 %all-to-all-start = ((bf16[32,8,6656]{2,1,0:T(8,128)(2,1)}), bf16[32,8,6656]{2,1,0:T(8,128)(2,1)S(1)}, u32[]{:S(2)}, u32[]{:S(2)}) async-start(bf16[32,8,6656]{2,1,0:T(8,128)(2,1)} %reshape.201), calls=%async_computation | async-start | bytes 6815744 | tf_op jit(solution)/shard_map/all_to_all | solution.py:195
Sparse Core Ops, SparseCore 0:
  25.5 362.8 all-reduce.2
where the time goes:
time: 569 us; the launch traced here: 558 us
  waiting for transfers between devices  297 us (52%)
  starting transfers between devices  81.7 us (14%)
  local copies, waits for them, and re-layouts  67.2 us (12%)
  Pallas kernels  63.5 us (11%)
  other arithmetic  30.3 us (5%)
  between operations  19.1 us (3%)
    ppermute x8, waiting for transfers between devices, passed_along(): lax.ppermute(value, axis, [(source, source + steps) for source in range(i...  227 us
    all_to_all x1, waiting for transfers between devices, body(): lax.all_to_all(arranged, ('dp', 'tile'), split_axis=0, concat_axis=0, til...  64.6 us
    all_to_all x1, starting transfers between devices, body(): lax.all_to_all(arranged, ('dp', 'tile'), split_axis=0, concat_axis=0, til...  53.5 us
    pallas_call x4, Pallas kernels, attend_near(): pl.pallas_call(near_kernel, grid_spec=pltpu.PrefetchScalarGridSpec(num_sc...  46.6 us
    ppermute x8, starting transfers between devices, passed_along(): lax.ppermute(value, axis, [(source, source + steps) for source in range(i...  28.2 us
    pallas_call x1, Pallas kernels, attend_thumb(): pl.pallas_call(thumb_kernel, grid_spec=pltpu.PrefetchScalarGridSpec(num_s...  17 us
  transfers between devices with their start and end apart: 10, of which 6 were waited for; matrix products, arithmetic and copies ran while one was open for 14% of the time, Pallas kernels for 8%

commit v1 on v0

--- a/solution.py
+++ b/solution.py
@@ -62,7 +62,11 @@
     top_ref[...] = top_in[0]
     sum_ref[...] = sum_in[0]
     merge_block(flags_ref[2], q_ref[...], k3, v3, acc_ref, top_ref, sum_ref)
-    o_ref[...] = (acc_ref[...] / sum_ref[...]).astype(o_ref.dtype)
+    attended = (acc_ref[...] / sum_ref[...]).astype(o_ref.dtype)
+    head = pl.program_id(0)
+    for patch in range(4):
+        column = pl.multiple_of(patch * HH + head * HD, HD)
+        o_ref[:, pl.ds(column, HD)] = attended[patch * SHUF : (patch + 1) * SHUF]
 
 
 def attend_near(flags, query_cols, blocks, first_head, head_count, state):
@@ -101,14 +105,14 @@
             num_scalar_prefetch=1,
             grid=(HEADS,),
             in_specs=[q_spec, q_spec, q_spec, q_spec, stat_spec, stat_spec],
-            out_specs=q_spec,
+            out_specs=pl.BlockSpec((SHUF, 4 * HH), lambda h, flags: (0, 0)),
             scratch_shapes=[
                 pltpu.VMEM((TOK, HD), jnp.float32),
                 pltpu.VMEM((TOK, 1), jnp.float32),
                 pltpu.VMEM((TOK, 1), jnp.float32),
             ],
         ),
-        out_shape=jax.ShapeDtypeStruct((TOK, HH), jnp.bfloat16),
+        out_shape=jax.ShapeDtypeStruct((SHUF, 4 * HH), jnp.bfloat16),
     )(flags, query_tile, thumb_keys, thumb_values, acc, top, totals)
 
 
@@ -163,6 +167,8 @@
             row_start % device_count,
             axis=1,
         )
+        .transpose(1, 0, 2)
+        .reshape(SHUF, 4, HH)
         .transpose(1, 0, 2)
         .reshape(TOK, HH)
     )

time: 569 us -> 560 us (0.984)
  local copies, waits for them, and re-layouts: 67.2 us -> 58.4 us
    reshape x1 -> x0, local copies, waits for them, and re-layouts: 6.69 us -> none  [body(): arranged = attended.reshape(device_count, per_peer, 4 * HH)]
where the time goes in v1:
time: 560 us; the launch traced here: 551 us
  waiting for transfers between devices  299 us (53%)
  starting transfers between devices  80.6 us (14%)
  Pallas kernels  63.7 us (11%)
  local copies, waits for them, and re-layouts  58.4 us (10%)
  other arithmetic  30.3 us (5%)
  between operations  19.1 us (3%)
    ppermute x8, waiting for transfers between devices, passed_along(): lax.ppermute(value, axis, [(source, source + steps) for source in range(i...  230 us
    all_to_all x1, waiting for transfers between devices, body(): lax.all_to_all(arranged, ('dp', 'tile'), split_axis=0, concat_axis=0, til...  64.6 us
    all_to_all x1, starting transfers between devices, body(): lax.all_to_all(arranged, ('dp', 'tile'), split_axis=0, concat_axis=0, til...  52.4 us
    pallas_call x4, Pallas kernels, attend_near(): pl.pallas_call(near_kernel, grid_spec=pltpu.PrefetchScalarGridSpec(num_sc...  46.6 us
    ppermute x8, starting transfers between devices, passed_along(): lax.ppermute(value, axis, [(source, source + steps) for source in range(i...  28.2 us
    pallas_call x1, Pallas kernels, attend_thumb(): pl.pallas_call(thumb_kernel, grid_spec=pltpu.PrefetchScalarGridSpec(num_s...  17.1 us
  transfers between devices with their start and end apart: 10, of which 6 were waited for; matrix products, arithmetic and copies ran while one was open for 14% of the time, Pallas kernels for 8%

profile of v1, /device:TPU:0, one launch (start us, length us, event | category | flops | bytes accessed | tf_op | source)
XLA Modules:
  0.0 550.8 jit_solution(501724535905258786)
XLA Ops:
  10.3 6.2 %collective-permute-start = (bf16[1024,1024]{1,0:T(8,128)(2,1)S(1)}, bf16[1024,1024]{1,0:T(8,128)(2,1)}, u32[]{:S(2)}, u32[]{:S(2)}) collective-permute-start(bf16[1024,1024]{1,0:T(8,128)(2,1)S(1)} %pad_maximum_fusion.k0.v0), channel_id=1, source_target_pairs={{0,1},{1,2},{2,3},{3,4},{4,5},{5,6},{6,7},{8,9},{9,10},{10,11},{11... | collective-permute-start | bytes 6291464 | tf_op jit(solution)/shard_map/ppermute | solution.py:21
  19.1 4.1 broadcast_select_fusion
  28.2 101.1 %collective-permute-done.k1.v1 = bf16[1024,1024]{1,0:T(8,128)(2,1)} collective-permute-done((bf16[1024,1024]{1,0:T(8,128)(2,1)S(1)}, bf16[1024,1024]{1,0:T(8,128)(2,1)}, u32[]{:S(2)}, u32[]{:S(2)}) %collective-permute-start) | collective-permute-done | bytes 2097184 | tf_op jit(solution)/shard_map/ppermute | solution.py:21
  129.3 5.9 %collective-permute-start.2 = (bf16[1024,1024]{1,0:T(8,128)(2,1)}, bf16[1024,1024]{1,0:T(8,128)(2,1)}, u32[]{:S(2)}, u32[]{:S(2)}) collective-permute-start(bf16[1024,1024]{1,0:T(8,128)(2,1)} %pad_maximum_fusion.1.k0.v0), channel_id=1, source_target_pairs={{0,1},{1,2},{2,3},{3,4},{4,5},{5,6},{6,7},{8,9},{9,10},{10,11},{11... | collective-permute-start | bytes 6291464 | tf_op jit(solution)/shard_map/ppermute | solution.py:21
  146.9 6.6 %reshape_reshape.6 = bf16[16,2,16,2,1664]{4,3,2,1,0:T(2,128)(2,1)S(1)} reshape(bf16[1,1,1024,1664]{3,2,1,0:T(8,128)(2,1)} %param.4) | data formatting | bytes 6815744 | tf_op jit(solution)/shard_map/reshape;reshape | solution.py:123
  153.5 4.3 copy.21
  157.8 7.3 %reshape_reshape.7 = bf16[8,32,6656]{2,1,0:T(8,128)(2,1)S(1)} reshape(bf16[16,16,2,2,1664]{4,3,2,1,0:T(2,128)(2,1)} %bitcast.76) | data formatting | bytes 6815744 | tf_op jit(solution)/shard_map/reshape;reshape | solution.py:166
  180.0 3.5 broadcast_10_top_prev_sum_prev.2.clone.top_prev
  190.1 13.5 %shard_map.46 = (f32[1024,1664]{1,0:T(8,128)}, f32[13,1024,1]{2,1,0:T(8,128)}, f32[13,1024,1]{2,1,0:T(8,128)}) custom-call(s32[3]{0:T(128)} %add_convert_fusion.flags_ref, bf16[1024,512]{1,0:T(8,128)(2,1)} %get-tuple-element.44.q_ref, bf16[1024,1024]{1,0:T(8,128)(2,1)} %copy-done.1, ...), custom_call_target="tpu_custom_call", output_to_operand_aliasing={{0}: (8, {}), {1}: (9, {}), {2}: (10, {})} | custom-call | tf_op jit(solution)/shard_map/pallas_call | solution.py:82
  203.6 36.5 %collective-permute-done.2.k1.v1 = bf16[1024,1024]{1,0:T(8,128)(2,1)} collective-permute-done((bf16[1024,1024]{1,0:T(8,128)(2,1)}, bf16[1024,1024]{1,0:T(8,128)(2,1)}, u32[]{:S(2)}, u32[]{:S(2)}) %collective-permute-start.2) | collective-permute-done | bytes 2097184 | tf_op jit(solution)/shard_map/ppermute | solution.py:21
  240.1 5.6 %collective-permute-start.4 = (bf16[1024,768]{1,0:T(8,128)(2,1)}, bf16[1024,768]{1,0:T(8,128)(2,1)}, u32[]{:S(2)}, u32[]{:S(2)}) collective-permute-start(bf16[1024,768]{1,0:T(8,128)(2,1)} %pad_maximum_fusion.2.k0.v0), channel_id=1, source_target_pairs={{0,1},{1,2},{2,3},{3,4},{4,5},{5,6},{6,7},{8,9},{9,10},{10,11},{11... | collective-permute-start | bytes 4718600 | tf_op jit(solution)/shard_map/ppermute | solution.py:21
  250.2 13.7 %shard_map.47 = (f32[1024,1664]{1,0:T(8,128)}, f32[13,1024,1]{2,1,0:T(8,128)}, f32[13,1024,1]{2,1,0:T(8,128)}) custom-call(s32[3]{0:T(128)} %add_convert_fusion.flags_ref, bf16[1024,512]{1,0:T(8,128)(2,1)} %get-tuple-element.43.q_ref, bf16[1024,1024]{1,0:T(8,128)(2,1)} %pad_maximum_fusion.1.k0.v0, ...), custom_call_target="tpu_custom_call", output_to_operand_aliasing={{0}: (8, {}), {1}: (9, {}), {2}: (10, {})} | custom-call | tf_op jit(solution)/shard_map/pallas_call | solution.py:82
  263.8 63.5 %collective-permute-done.4.k1.v1 = bf16[1024,768]{1,0:T(8,128)(2,1)} collective-permute-done((bf16[1024,768]{1,0:T(8,128)(2,1)}, bf16[1024,768]{1,0:T(8,128)(2,1)}, u32[]{:S(2)}, u32[]{:S(2)}) %collective-permute-start.4) | collective-permute-done | bytes 1572896 | tf_op jit(solution)/shard_map/ppermute | solution.py:21
  327.4 5.4 collective-permute-start.6
  335.8 10.9 %shard_map.48 = (f32[1024,1664]{1,0:T(8,128)}, f32[13,1024,1]{2,1,0:T(8,128)}, f32[13,1024,1]{2,1,0:T(8,128)}) custom-call(s32[3]{0:T(128)} %add_convert_fusion.flags_ref, bf16[1024,384]{1,0:T(8,128)(2,1)} %slice.143.q_ref, bf16[1024,768]{1,0:T(8,128)(2,1)} %pad_maximum_fusion.2.k0.v0, ...), custom_call_target="tpu_custom_call", output_to_operand_aliasing={{0}: (8, {}), {1}: (9, {}), {2}: (10, {})} | custom-call | tf_op jit(solution)/shard_map/pallas_call | solution.py:82
  346.7 28.5 %collective-permute-done.6.k1.v1 = bf16[1024,512]{1,0:T(8,128)(2,1)} collective-permute-done((bf16[1024,512]{1,0:T(8,128)(2,1)}, bf16[1024,512]{1,0:T(8,128)(2,1)}, u32[]{:S(2)}, u32[]{:S(2)}) %collective-permute-start.6) | collective-permute-done | bytes 1048608 | tf_op jit(solution)/shard_map/ppermute | solution.py:21
  375.3 8.5 %shard_map.49 = (f32[1024,1664]{1,0:T(8,128)}, f32[13,1024,1]{2,1,0:T(8,128)}, f32[13,1024,1]{2,1,0:T(8,128)}) custom-call(s32[3]{0:T(128)} %add_convert_fusion.flags_ref, bf16[1024,256]{1,0:T(8,128)(2,1)} %slice.132.q_ref, bf16[1024,512]{1,0:T(8,128)(2,1)} %pad_maximum_fusion.3.k0.v0, ...), custom_call_target="tpu_custom_call", output_to_operand_aliasing={{0}: (8, {}), {1}: (9, {}), {2}: (10, {})} | custom-call | tf_op jit(solution)/shard_map/pallas_call | solution.py:82
  383.8 4.6 all-reduce.3.cloned.1.call-done
  388.4 17.1 %shard_map.50 = bf16[256,6656]{1,0:T(8,128)(2,1)} custom-call(s32[3]{0:T(128)} %add_convert_fusion.flags_ref, bf16[1024,1664]{1,0:T(8,128)(2,1)} %bitcast.68, bf16[1024,1664]{1,0:T(8,128)(2,1)} %get-tuple-element.35.k3, bf16[1024,1664]{1,0:T(8,128)(2,1)} %get-tuple-element.36.v3, f32[1024,1664]{1,0:T(8,128)} %get-tuple-element.32.acc_in, ...), custom_call_target="tpu_custom_call" | custom-call | tf_op jit(solution)/shard_map/pallas_call | solution.py:102
  405.5 52.4 %all-to-all-start = ((bf16[32,8,6656]{2,1,0:T(8,128)(2,1)}), bf16[32,8,6656]{2,1,0:T(8,128)(2,1)S(1)}, u32[]{:S(2)}, u32[]{:S(2)}) async-start(bf16[32,8,6656]{2,1,0:T(8,128)(2,1)} %bitcast.69), calls=%async_computation | async-start | bytes 6815744 | tf_op jit(solution)/shard_map/all_to_all | solution.py:201
  458.6 7.6 %and_or_fusion = (pred[32]{0:T(512)(128)(4,1)S(1)}, s32[32,1]{0,1:T(1,128)S(1)}, s32[32]{0:T(128)S(1)}, pred[32]{0:T(512)(128)(4,1)S(1)}) fusion(s32[]{:T(128)} %bitcast.8, s32[]{:T(128)} %bitcast.7, s32[]{:T(128)} %bitcast.6, s32[]{:T(128)} %bitcast.5, s32[]{:T(128)} %bitcast.3, s32[]{:T(128)} %bitcast.2, s32[]{:T(128)} %bitcast.1, s32[]{:T(128)} %bitcast, ...), kind=kLoop, calls=%fused_computation.31 | loop fusion | flops 1120 | bytes 368 | tf_op jit(solution)/shard_map/or | solution.py:208
  466.2 5.1 and_select_fusion
  471.5 64.6 %all-to-all-done = bf16[32,8,6656]{2,1,0:T(8,128)(2,1)S(1)} async-done(((bf16[32,8,6656]{2,1,0:T(8,128)(2,1)}), bf16[32,8,6656]{2,1,0:T(8,128)(2,1)S(1)}, u32[]{:S(2)}, u32[]{:S(2)}) %all-to-all-start) | async-done | bytes 3407904 | tf_op jit(solution)/shard_map/all_to_all | solution.py:201
  536.1 7.4 %scatter_custom_fusion = bf16[288,6656]{1,0:T(8,128)(2,1)} fusion(s32[256]{0:T(256)S(1)} %bitcast.78, bf16[32,8,6656]{2,1,0:T(8,128)(2,1)S(1)} %all-to-all-done, bf16[]{:T(256)} %constant.98.clone.1), kind=kCustom, calls=%fused_computation.5 | custom fusion | bytes 7241730 | tf_op jit(solution)/shard_map/scatter | solution.py:219
  (49 shorter events, 47.9 us)
Async XLA Ops:
  6.5 381.8 %all-reduce.3.cloned.1.call-start = ((), (), s32[]{:S(2)}) async-start(), calls=%async_computation.1 | async-start | bytes 13631488 | tf_op jit(solution)/shard_map/psum | solution.py:177
  10.0 7.8 %copy-start.3 = (s32[4,5]{1,0:T(4,128)S(1)}, s32[4,5]{1,0:T(4,128)}, u32[]{:S(2)}) copy-start(s32[4,5]{1,0:T(4,128)} %param.7) | copy-start | bytes 244
  10.3 12.9 %copy-start.1 = (bf16[1024,1024]{1,0:T(8,128)(2,1)}, bf16[1024,1024]{1,0:T(8,128)(2,1)S(1)}, u32[]{:S(2)}) copy-start(bf16[1024,1024]{1,0:T(8,128)(2,1)S(1)} %pad_maximum_fusion.k0.v0) | copy-start | bytes 6291460
  10.3 119.0 %collective-permute-start = (bf16[1024,1024]{1,0:T(8,128)(2,1)S(1)}, bf16[1024,1024]{1,0:T(8,128)(2,1)}, u32[]{:S(2)}, u32[]{:S(2)}) collective-permute-start(bf16[1024,1024]{1,0:T(8,128)(2,1)S(1)} %pad_maximum_fusion.k0.v0), channel_id=1, source_target_pairs={{0,1},{1,2},{2,3},{3,4},{4,5},{5,6},{6,7},{8,9},{9,10},{10,11},{11... | collective-permute-start | bytes 6291464 | tf_op jit(solution)/shard_map/ppermute | solution.py:21
  16.5 112.8 %collective-permute-start.1 = (bf16[1024,1024]{1,0:T(8,128)(2,1)S(1)}, bf16[1024,1024]{1,0:T(8,128)(2,1)}, u32[]{:S(2)}, u32[]{:S(2)}) collective-permute-start(bf16[1024,1024]{1,0:T(8,128)(2,1)S(1)} %pad_maximum_fusion.k0.v0), channel_id=1, source_target_pairs={{1,0},{2,1},{3,2},{4,3},{5,4},{6,5},{7,6},{9,8},{10,9},{11,10},{12... | collective-permute-start | bytes 6291464 | tf_op jit(solution)/shard_map/ppermute | solution.py:21
  19.1 4.1 copy-start.2
  129.3 110.8 %collective-permute-start.2 = (bf16[1024,1024]{1,0:T(8,128)(2,1)}, bf16[1024,1024]{1,0:T(8,128)(2,1)}, u32[]{:S(2)}, u32[]{:S(2)}) collective-permute-start(bf16[1024,1024]{1,0:T(8,128)(2,1)} %pad_maximum_fusion.1.k0.v0), channel_id=1, source_target_pairs={{0,1},{1,2},{2,3},{3,4},{4,5},{5,6},{6,7},{8,9},{9,10},{10,11},{11... | collective-permute-start | bytes 6291464 | tf_op jit(solution)/shard_map/ppermute | solution.py:21
  135.1 104.9 %collective-permute-start.3 = (bf16[1024,1024]{1,0:T(8,128)(2,1)}, bf16[1024,1024]{1,0:T(8,128)(2,1)}, u32[]{:S(2)}, u32[]{:S(2)}) collective-permute-start(bf16[1024,1024]{1,0:T(8,128)(2,1)} %pad_maximum_fusion.1.k0.v0), channel_id=1, source_target_pairs={{1,0},{2,1},{3,2},{4,3},{5,4},{6,5},{7,6},{9,8},{10,9},{11,10},{12... | collective-permute-start | bytes 6291464 | tf_op jit(solution)/shard_map/ppermute | solution.py:21
  174.1 160.9 %copy-start = (bf16[4,256,1664]{2,1,0:T(8,128)(2,1)}, bf16[4,256,1664]{2,1,0:T(8,128)(2,1)S(1)}, u32[]{:S(2)}) copy-start(bf16[4,256,1664]{2,1,0:T(8,128)(2,1)S(1)} %copy.19) | copy-start | bytes 10223620
  240.1 87.3 %collective-permute-start.4 = (bf16[1024,768]{1,0:T(8,128)(2,1)}, bf16[1024,768]{1,0:T(8,128)(2,1)}, u32[]{:S(2)}, u32[]{:S(2)}) collective-permute-start(bf16[1024,768]{1,0:T(8,128)(2,1)} %pad_maximum_fusion.2.k0.v0), channel_id=1, source_target_pairs={{0,1},{1,2},{2,3},{3,4},{4,5},{5,6},{6,7},{8,9},{9,10},{10,11},{11... | collective-permute-start | bytes 4718600 | tf_op jit(solution)/shard_map/ppermute | solution.py:21
  245.7 81.7 %collective-permute-start.5 = (bf16[1024,768]{1,0:T(8,128)(2,1)}, bf16[1024,768]{1,0:T(8,128)(2,1)}, u32[]{:S(2)}, u32[]{:S(2)}) collective-permute-start(bf16[1024,768]{1,0:T(8,128)(2,1)} %pad_maximum_fusion.2.k0.v0), channel_id=1, source_target_pairs={{1,0},{2,1},{3,2},{4,3},{5,4},{6,5},{7,6},{9,8},{10,9},{11,10},{12... | collective-permute-start | bytes 4718600 | tf_op jit(solution)/shard_map/ppermute | solution.py:21
  327.4 47.9 %collective-permute-start.6 = (bf16[1024,512]{1,0:T(8,128)(2,1)}, bf16[1024,512]{1,0:T(8,128)(2,1)}, u32[]{:S(2)}, u32[]{:S(2)}) collective-permute-start(bf16[1024,512]{1,0:T(8,128)(2,1)} %pad_maximum_fusion.3.k0.v0), channel_id=1, source_target_pairs={{0,1},{1,2},{2,3},{3,4},{4,5},{5,6},{6,7},{8,9},{9,10},{10,11},{11... | collective-permute-start | bytes 3145736 | tf_op jit(solution)/shard_map/ppermute | solution.py:21
  332.8 42.5 %collective-permute-start.7 = (bf16[1024,512]{1,0:T(8,128)(2,1)}, bf16[1024,512]{1,0:T(8,128)(2,1)}, u32[]{:S(2)}, u32[]{:S(2)}) collective-permute-start(bf16[1024,512]{1,0:T(8,128)(2,1)} %pad_maximum_fusion.3.k0.v0), channel_id=1, source_target_pairs={{1,0},{2,1},{3,2},{4,3},{5,4},{6,5},{7,6},{9,8},{10,9},{11,10},{12... | collective-permute-start | bytes 3145736 | tf_op jit(solution)/shard_map/ppermute | solution.py:21
  405.5 130.6 %all-to-all-start = ((bf16[32,8,6656]{2,1,0:T(8,128)(2,1)}), bf16[32,8,6656]{2,1,0:T(8,128)(2,1)S(1)}, u32[]{:S(2)}, u32[]{:S(2)}) async-start(bf16[32,8,6656]{2,1,0:T(8,128)(2,1)} %bitcast.69), calls=%async_computation | async-start | bytes 6815744 | tf_op jit(solution)/shard_map/all_to_all | solution.py:201
Sparse Core Ops, SparseCore 0:
  25.5 362.8 all-reduce.2

commit v2 on v1

--- a/solution.py
+++ b/solution.py
@@ -96,14 +96,14 @@
     )(flags, query_cols, *operands, *state)
 
 
-def attend_thumb(flags, query_tile, thumb_keys, thumb_values, acc, top, totals):
+def attend_thumb(flags, query_tile, thumb_keys, thumb_values, acc, top, totals, head_count):
     q_spec = pl.BlockSpec((TOK, HD), lambda h, flags: (0, h))
     stat_spec = pl.BlockSpec((1, TOK, 1), lambda h, flags: (h, 0, 0))
     return pl.pallas_call(
         thumb_kernel,
         grid_spec=pltpu.PrefetchScalarGridSpec(
             num_scalar_prefetch=1,
-            grid=(HEADS,),
+            grid=(head_count,),
             in_specs=[q_spec, q_spec, q_spec, q_spec, stat_spec, stat_spec],
             out_specs=pl.BlockSpec((SHUF, 4 * HH), lambda h, flags: (0, 0)),
             scratch_shapes=[
@@ -114,6 +114,51 @@
         ),
         out_shape=jax.ShapeDtypeStruct((SHUF, 4 * HH), jnp.bfloat16),
     )(flags, query_tile, thumb_keys, thumb_values, acc, top, totals)
+
+
+def last_kernel(flags_ref, q_ref, k0, v0, k1, v1, k2, v2, k3, v3, out_prev, o_ref, held_ref, acc_ref, top_ref, sum_ref):
+    @pl.when(pl.program_id(1) == 0)
+    def _():
+        query = q_ref[...]
+        numerator, largest, totals = block_terms(query, k0, v0)
+        acc_ref[...] = numerator
+        top_ref[...] = largest
+        sum_ref[...] = totals
+        for index, (k_ref, v_ref) in enumerate(((k1, v1), (k2, v2), (k3, v3))):
+            merge_block(flags_ref[index], query, k_ref, v_ref, acc_ref, top_ref, sum_ref)
+        held_ref[...] = (acc_ref[...] / sum_ref[...]).astype(held_ref.dtype)
+
+    patch = pl.program_id(1)
+    o_ref[...] = held_ref[pl.ds(pl.multiple_of(patch * SHUF, SHUF), SHUF)]
+
+
+def attend_last(flags, query_cols, blocks, thumb_keys, thumb_values, first_head, head_count, out_prev):
+    q_spec = pl.BlockSpec((TOK, HD), lambda h, p, flags: (0, h))
+    v_spec = pl.BlockSpec((TOK, HD), lambda h, p, flags: (0, head_count + h))
+    t_spec = pl.BlockSpec((TOK, HD), lambda h, p, flags: (0, first_head + h))
+    o_spec = pl.BlockSpec((SHUF, HD), lambda h, p, flags: (0, p * HEADS + first_head + h))
+    operands = []
+    for both in blocks:
+        operands += [both, both]
+    count = 1 + len(operands) + 2
+    return pl.pallas_call(
+        last_kernel,
+        grid_spec=pltpu.PrefetchScalarGridSpec(
+            num_scalar_prefetch=1,
+            grid=(head_count, 4),
+            in_specs=[q_spec] + [q_spec, v_spec] * len(blocks) + [t_spec, t_spec]
+            + [pl.BlockSpec(memory_space=pl.ANY)],
+            out_specs=o_spec,
+            scratch_shapes=[
+                pltpu.VMEM((TOK, HD), jnp.bfloat16),
+                pltpu.VMEM((TOK, HD), jnp.float32),
+                pltpu.VMEM((TOK, 1), jnp.float32),
+                pltpu.VMEM((TOK, 1), jnp.float32),
+            ],
+        ),
+        out_shape=jax.ShapeDtypeStruct((SHUF, 4 * HH), jnp.bfloat16),
+        input_output_aliases={count + 1: 0},
+    )(flags, query_cols, *operands, thumb_keys, thumb_values, out_prev)
 
 
 def pixel_shuffle(attended):
@@ -183,7 +228,8 @@
     )
     arrived_last = None
     state_before = None
-    for first_head, end_head in HEAD_CHUNKS:
+    *near_chunks, (last_first, last_end) = HEAD_CHUNKS
+    for first_head, end_head in near_chunks:
         head_count = end_head - first_head
         cols = slice(first_head * HD, end_head * HD)
         own = jnp.concatenate([key_tile[:, cols], value_tile[:, cols]], axis=1)
@@ -196,7 +242,24 @@
         state = attend_near(
             flags, query_tile[:, cols], (own, left, right), first_head, head_count, state
         )
-    attended = attend_thumb(flags, query_tile, thumb_keys, thumb_values, *state)
+    cols = slice(last_first * HD, last_end * HD)
+    own = jnp.concatenate([key_tile[:, cols], value_tile[:, cols]], axis=1)
+    arrived_last, state_before, thumb_keys, thumb_values, own = lax.optimization_barrier(
+        (arrived_last, state_before, thumb_keys, thumb_values, own)
+    )
+    left = passed_along(own, "tile", 1)
+    right = passed_along(own, "tile", -1)
+    attended = attend_thumb(flags, query_tile, thumb_keys, thumb_values, *state, last_first)
+    attended = attend_last(
+        flags,
+        query_tile[:, cols],
+        (own, left, right),
+        thumb_keys,
+        thumb_values,
+        last_first,
+        last_end - last_first,
+        attended,
+    )
     arranged = attended.reshape(device_count, per_peer, 4 * HH)
     arrived = lax.all_to_all(arranged, ("dp", "tile"), split_axis=0, concat_axis=0, tiled=True)
     own_rank = page_index * slot_count + slot_index

time: 560 us -> 571 us (1.020); the launches traced: 551 us -> 573 us
  waiting for transfers between devices: 299 us -> 337 us
  starting transfers between devices: 80.6 us -> 65.4 us
    psum x1, waiting for transfers between devices: 4.6 us -> 45.2 us  [body(): lax.psum(jnp.where(mine, key_tile, jnp.zeros_like(key_tile)), 'tile')]
    all_to_all x1, starting transfers between devices: 52.4 us -> 37.6 us  [body(): lax.all_to_all(arranged, ('dp', 'tile'), split_axis=0, concat_axis=0, til...]
    pallas_call x0 -> x1, Pallas kernels: none -> 11.5 us  [attend_last(): pl.pallas_call(last_kernel, grid_spec=pltpu.PrefetchScalarGridSpec(num_sc...]
    pallas_call x4 -> x3, Pallas kernels: 46.6 us -> 38.1 us  [attend_near(): pl.pallas_call(near_kernel, grid_spec=pltpu.PrefetchScalarGridSpec(num_sc...]
  transfers between devices with their start and end apart: 10 -> 10, of which waited for: 6 -> 6; matrix products, arithmetic and copies ran while one was open for 14% -> 12% of each run, Pallas kernels for 8% -> 9%
where the time goes in v2:
time: 571 us; the launch traced here: 573 us
  waiting for transfers between devices  337 us (59%)
  starting transfers between devices  65.4 us (11%)
  Pallas kernels  64.5 us (11%)
  local copies, waits for them, and re-layouts  57 us (10%)
  other arithmetic  29.8 us (5%)
  between operations  19 us (3%)
    ppermute x8, waiting for transfers between devices, passed_along(): lax.ppermute(value, axis, [(source, source + steps) for source in range(i...  227 us
    all_to_all x1, waiting for transfers between devices, body(): lax.all_to_all(arranged, ('dp', 'tile'), split_axis=0, concat_axis=0, til...  64.7 us
    psum x1, waiting for transfers between devices, body(): lax.psum(jnp.where(mine, key_tile, jnp.zeros_like(key_tile)), 'tile')  45.2 us
    pallas_call x3, Pallas kernels, attend_near(): pl.pallas_call(near_kernel, grid_spec=pltpu.PrefetchScalarGridSpec(num_sc...  38.1 us
    all_to_all x1, starting transfers between devices, body(): lax.all_to_all(arranged, ('dp', 'tile'), split_axis=0, concat_axis=0, til...  37.6 us
    ppermute x8, starting transfers between devices, passed_along(): lax.ppermute(value, axis, [(source, source + steps) for source in range(i...  27.8 us
    pallas_call x1, Pallas kernels, attend_thumb(): pl.pallas_call(thumb_kernel, grid_spec=pltpu.PrefetchScalarGridSpec(num_s...  15 us
    pallas_call x1, Pallas kernels, attend_last(): pl.pallas_call(last_kernel, grid_spec=pltpu.PrefetchScalarGridSpec(num_sc...  11.5 us
  transfers between devices with their start and end apart: 10, of which 6 were waited for; matrix products, arithmetic and copies ran while one was open for 12% of the time, Pallas kernels for 9%

profile of v2, /device:TPU:0, one launch (start us, length us, event | category | flops | bytes accessed | tf_op | source)
XLA Modules:
  0.0 572.8 jit_solution(10622201484175550328)
XLA Ops:
  8.7 4.1 broadcast_select_fusion
  17.1 5.0 collective-permute-start
  25.0 111.1 %collective-permute-done.k1.v1 = bf16[1024,1024]{1,0:T(8,128)(2,1)S(1)} collective-permute-done((bf16[1024,1024]{1,0:T(8,128)(2,1)S(1)}, bf16[1024,1024]{1,0:T(8,128)(2,1)S(1)}, u32[]{:S(2)}, u32[]{:S(2)}) %collective-permute-start) | collective-permute-done | bytes 2097184 | tf_op jit(solution)/shard_map/ppermute | solution.py:21
  137.4 5.8 %collective-permute-start.2 = (bf16[1024,1024]{1,0:T(8,128)(2,1)}, bf16[1024,1024]{1,0:T(8,128)(2,1)}, u32[]{:S(2)}, u32[]{:S(2)}) collective-permute-start(bf16[1024,1024]{1,0:T(8,128)(2,1)} %pad_maximum_fusion.1.k0.v0), channel_id=1, source_target_pairs={{0,1},{1,2},{2,3},{3,4},{4,5},{5,6},{6,7},{8,9},{9,10},{10,11},{11... | collective-permute-start | bytes 6291464 | tf_op jit(solution)/shard_map/ppermute | solution.py:21
  153.9 6.6 %reshape_reshape.6 = bf16[16,2,16,2,1664]{4,3,2,1,0:T(2,128)(2,1)S(1)} reshape(bf16[1,1,1024,1664]{3,2,1,0:T(8,128)(2,1)} %param.4) | data formatting | bytes 6815744 | tf_op jit(solution)/shard_map/reshape;reshape | solution.py:168
  160.6 4.3 copy.19
  164.9 7.3 %reshape_reshape.7 = bf16[8,32,6656]{2,1,0:T(8,128)(2,1)S(1)} reshape(bf16[16,16,2,2,1664]{4,3,2,1,0:T(2,128)(2,1)} %bitcast.76) | data formatting | bytes 6815744 | tf_op jit(solution)/shard_map/reshape;reshape | solution.py:211
  187.1 3.5 broadcast_10_top_prev_sum_prev.2.clone.top_prev
  197.3 13.5 %shard_map.46 = (f32[1024,1664]{1,0:T(8,128)}, f32[13,1024,1]{2,1,0:T(8,128)}, f32[13,1024,1]{2,1,0:T(8,128)}) custom-call(s32[3]{0:T(128)} %add_convert_fusion.flags_ref, bf16[1024,512]{1,0:T(8,128)(2,1)} %get-tuple-element.42.q_ref, bf16[1024,1024]{1,0:T(8,128)(2,1)} %copy-done.1, ...), custom_call_target="tpu_custom_call", output_to_operand_aliasing={{0}: (8, {}), {1}: (9, {}), {2}: (10, {})} | custom-call | tf_op jit(solution)/shard_map/pallas_call | solution.py:82
  210.8 41.7 %collective-permute-done.2.k1.v1 = bf16[1024,1024]{1,0:T(8,128)(2,1)} collective-permute-done((bf16[1024,1024]{1,0:T(8,128)(2,1)}, bf16[1024,1024]{1,0:T(8,128)(2,1)}, u32[]{:S(2)}, u32[]{:S(2)}) %collective-permute-start.2) | collective-permute-done | bytes 2097184 | tf_op jit(solution)/shard_map/ppermute | solution.py:21
  252.4 5.6 collective-permute-start.4
  262.5 13.7 %shard_map.47 = (f32[1024,1664]{1,0:T(8,128)}, f32[13,1024,1]{2,1,0:T(8,128)}, f32[13,1024,1]{2,1,0:T(8,128)}) custom-call(s32[3]{0:T(128)} %add_convert_fusion.flags_ref, bf16[1024,512]{1,0:T(8,128)(2,1)} %get-tuple-element.41.q_ref, bf16[1024,1024]{1,0:T(8,128)(2,1)} %pad_maximum_fusion.1.k0.v0, ...), custom_call_target="tpu_custom_call", output_to_operand_aliasing={{0}: (8, {}), {1}: (9, {}), {2}: (10, {})} | custom-call | tf_op jit(solution)/shard_map/pallas_call | solution.py:82
  276.2 59.3 %collective-permute-done.4.k1.v1 = bf16[1024,768]{1,0:T(8,128)(2,1)} collective-permute-done((bf16[1024,768]{1,0:T(8,128)(2,1)}, bf16[1024,768]{1,0:T(8,128)(2,1)}, u32[]{:S(2)}, u32[]{:S(2)}) %collective-permute-start.4) | collective-permute-done | bytes 1572896 | tf_op jit(solution)/shard_map/ppermute | solution.py:21
  335.5 45.2 %all-reduce.3.cloned.1.call-done = (bf16[1024,1664]{1,0:T(8,128)(2,1)}, bf16[1024,1664]{1,0:T(8,128)(2,1)}) async-done(((bf16[1024,1664]{1,0:T(8,128)(2,1)}, bf16[1024,1664]{1,0:T(8,128)(2,1)}), (bf16[1024,1664]{1,0:T(8,128)(2,1)}, bf16[1024,1664]{1,0:T(8,128)(2,1)})) %all-reduce.3.cloned.1.call-update) | async-done | bytes 6815760 | tf_op jit(solution)/shard_map/psum | solution.py:222
  380.7 6.2 %collective-permute-start.6 = (bf16[1024,512]{1,0:T(8,128)(2,1)}, bf16[1024,512]{1,0:T(8,128)(2,1)}, u32[]{:S(2)}, u32[]{:S(2)}) collective-permute-start(bf16[1024,512]{1,0:T(8,128)(2,1)} %pad_maximum_fusion.3.k0.v0), channel_id=1, source_target_pairs={{0,1},{1,2},{2,3},{3,4},{4,5},{5,6},{6,7},{8,9},{9,10},{10,11},{11... | collective-permute-start | bytes 3145736 | tf_op jit(solution)/shard_map/ppermute | solution.py:21
  390.0 10.9 %shard_map.48 = (f32[1024,1664]{1,0:T(8,128)}, f32[13,1024,1]{2,1,0:T(8,128)}, f32[13,1024,1]{2,1,0:T(8,128)}) custom-call(s32[3]{0:T(128)} %add_convert_fusion.flags_ref, bf16[1024,384]{1,0:T(8,128)(2,1)} %slice.143.q_ref, bf16[1024,768]{1,0:T(8,128)(2,1)} %pad_maximum_fusion.2.k0.v0, ...), custom_call_target="tpu_custom_call", output_to_operand_aliasing={{0}: (8, {}), {1}: (9, {}), {2}: (10, {})} | custom-call | tf_op jit(solution)/shard_map/pallas_call | solution.py:82
  400.9 15.0 %shard_map.49.out_prev = bf16[256,6656]{1,0:T(8,128)(2,1)} custom-call(s32[3]{0:T(128)} %add_convert_fusion.flags_ref, bf16[1024,1664]{1,0:T(8,128)(2,1)} %bitcast.68, bf16[1024,1664]{1,0:T(8,128)(2,1)} %get-tuple-element.28.k3, bf16[1024,1664]{1,0:T(8,128)(2,1)} %get-tuple-element.29.v3, f32[1024,1664]{1,0:T(8,128)} %get-tuple-element.30.acc_in, ...), custom_call_target="tpu_custom_call" | custom-call | tf_op jit(solution)/shard_map/pallas_call | solution.py:102
  415.8 15.1 %collective-permute-done.6.k1.v1 = bf16[1024,512]{1,0:T(8,128)(2,1)} collective-permute-done((bf16[1024,512]{1,0:T(8,128)(2,1)}, bf16[1024,512]{1,0:T(8,128)(2,1)}, u32[]{:S(2)}, u32[]{:S(2)}) %collective-permute-start.6) | collective-permute-done | bytes 1048608 | tf_op jit(solution)/shard_map/ppermute | solution.py:21
  431.0 11.5 %shard_map.50 = bf16[256,6656]{1,0:T(8,128)(2,1)} custom-call(s32[3]{0:T(128)} %add_convert_fusion.flags_ref, bf16[1024,256]{1,0:T(8,128)(2,1)} %slice.132.q_ref, bf16[1024,512]{1,0:T(8,128)(2,1)} %pad_maximum_fusion.3.k0.v0, bf16[1024,512]{1,0:T(8,128)(2,1)} %pad_maximum_fusion.3.k0.v0, ...), custom_call_target="tpu_custom_call", output_to_operand_aliasing={{}: (10, {})} | custom-call | tf_op jit(solution)/shard_map/pallas_call | solution.py:144
  442.5 37.6 %all-to-all-start = ((bf16[32,8,6656]{2,1,0:T(8,128)(2,1)}), bf16[32,8,6656]{2,1,0:T(8,128)(2,1)S(1)}, u32[]{:S(2)}, u32[]{:S(2)}) async-start(bf16[32,8,6656]{2,1,0:T(8,128)(2,1)} %bitcast.69), calls=%async_computation | async-start | bytes 6815744 | tf_op jit(solution)/shard_map/all_to_all | solution.py:264
  480.8 7.5 %and_or_fusion = (pred[32]{0:T(512)(128)(4,1)S(1)}, s32[32,1]{0,1:T(1,128)S(1)}, s32[32]{0:T(128)S(1)}, pred[32]{0:T(512)(128)(4,1)S(1)}) fusion(s32[]{:T(128)} %bitcast.8, s32[]{:T(128)} %bitcast.7, s32[]{:T(128)} %bitcast.6, s32[]{:T(128)} %bitcast.5, s32[]{:T(128)} %bitcast.3, s32[]{:T(128)} %bitcast.2, s32[]{:T(128)} %bitcast.1, s32[]{:T(128)} %bitcast, ...), kind=kLoop, calls=%fused_computation.31 | loop fusion | flops 1120 | bytes 368 | tf_op jit(solution)/shard_map/or | solution.py:271
  488.4 5.1 and_select_fusion
  493.7 64.7 %all-to-all-done = bf16[32,8,6656]{2,1,0:T(8,128)(2,1)S(1)} async-done(((bf16[32,8,6656]{2,1,0:T(8,128)(2,1)}), bf16[32,8,6656]{2,1,0:T(8,128)(2,1)S(1)}, u32[]{:S(2)}, u32[]{:S(2)}) %all-to-all-start) | async-done | bytes 3407904 | tf_op jit(solution)/shard_map/all_to_all | solution.py:264
  558.3 7.4 %scatter_custom_fusion = bf16[288,6656]{1,0:T(8,128)(2,1)} fusion(s32[256]{0:T(256)S(1)} %bitcast.78, bf16[32,8,6656]{2,1,0:T(8,128)(2,1)S(1)} %all-to-all-done, bf16[]{:T(256)} %constant.98.clone.1), kind=kCustom, calls=%fused_computation.5 | custom fusion | bytes 7241730 | tf_op jit(solution)/shard_map/scatter | solution.py:282
  (53 shorter events, 46.2 us)
Async XLA Ops:
  6.5 374.1 %all-reduce.3.cloned.1.call-start = ((), (), s32[]{:S(2)}) async-start(), calls=%async_computation.1 | async-start | bytes 13631488 | tf_op jit(solution)/shard_map/psum | solution.py:222
  8.7 4.1 copy-start.2
  17.1 5.0 copy-start.1
  17.1 119.0 %collective-permute-start = (bf16[1024,1024]{1,0:T(8,128)(2,1)S(1)}, bf16[1024,1024]{1,0:T(8,128)(2,1)S(1)}, u32[]{:S(2)}, u32[]{:S(2)}) collective-permute-start(bf16[1024,1024]{1,0:T(8,128)(2,1)S(1)} %pad_maximum_fusion.k0.v0), channel_id=1, source_target_pairs={{0,1},{1,2},{2,3},{3,4},{4,5},{5,6},{6,7},{8,9},{9,10},{10,11},{11... | collective-permute-start | bytes 6291464 | tf_op jit(solution)/shard_map/ppermute | solution.py:21
  22.1 114.0 %collective-permute-start.1 = (bf16[1024,1024]{1,0:T(8,128)(2,1)S(1)}, bf16[1024,1024]{1,0:T(8,128)(2,1)S(1)}, u32[]{:S(2)}, u32[]{:S(2)}) collective-permute-start(bf16[1024,1024]{1,0:T(8,128)(2,1)S(1)} %pad_maximum_fusion.k0.v0), channel_id=1, source_target_pairs={{1,0},{2,1},{3,2},{4,3},{5,4},{6,5},{7,6},{9,8},{10,9},{11,10},{12... | collective-permute-start | bytes 6291464 | tf_op jit(solution)/shard_map/ppermute | solution.py:21
  136.0 1.4 copy-start.3
  137.4 5.8 %copy-start.4 = (bf16[1024,1024]{1,0:T(8,128)(2,1)}, bf16[1024,1024]{1,0:T(8,128)(2,1)S(1)}, u32[]{:S(2)}) copy-start(bf16[1024,1024]{1,0:T(8,128)(2,1)S(1)} %collective-permute-done.1.k2.v2) | copy-start | bytes 6291460
  137.4 115.0 %collective-permute-start.2 = (bf16[1024,1024]{1,0:T(8,128)(2,1)}, bf16[1024,1024]{1,0:T(8,128)(2,1)}, u32[]{:S(2)}, u32[]{:S(2)}) collective-permute-start(bf16[1024,1024]{1,0:T(8,128)(2,1)} %pad_maximum_fusion.1.k0.v0), channel_id=1, source_target_pairs={{0,1},{1,2},{2,3},{3,4},{4,5},{5,6},{6,7},{8,9},{9,10},{10,11},{11... | collective-permute-start | bytes 6291464 | tf_op jit(solution)/shard_map/ppermute | solution.py:21
  143.2 109.3 %collective-permute-start.3 = (bf16[1024,1024]{1,0:T(8,128)(2,1)}, bf16[1024,1024]{1,0:T(8,128)(2,1)}, u32[]{:S(2)}, u32[]{:S(2)}) collective-permute-start(bf16[1024,1024]{1,0:T(8,128)(2,1)} %pad_maximum_fusion.1.k0.v0), channel_id=1, source_target_pairs={{1,0},{2,1},{3,2},{4,3},{5,4},{6,5},{7,6},{9,8},{10,9},{11,10},{12... | collective-permute-start | bytes 6291464 | tf_op jit(solution)/shard_map/ppermute | solution.py:21
  181.2 207.9 %copy-start = (bf16[4,256,1664]{2,1,0:T(8,128)(2,1)}, bf16[4,256,1664]{2,1,0:T(8,128)(2,1)S(1)}, u32[]{:S(2)}) copy-start(bf16[4,256,1664]{2,1,0:T(8,128)(2,1)S(1)} %copy.17) | copy-start | bytes 10223620
  252.4 83.1 %collective-permute-start.4 = (bf16[1024,768]{1,0:T(8,128)(2,1)}, bf16[1024,768]{1,0:T(8,128)(2,1)}, u32[]{:S(2)}, u32[]{:S(2)}) collective-permute-start(bf16[1024,768]{1,0:T(8,128)(2,1)} %pad_maximum_fusion.2.k0.v0), channel_id=1, source_target_pairs={{0,1},{1,2},{2,3},{3,4},{4,5},{5,6},{6,7},{8,9},{9,10},{10,11},{11... | collective-permute-start | bytes 4718600 | tf_op jit(solution)/shard_map/ppermute | solution.py:21
  258.0 77.5 %collective-permute-start.5 = (bf16[1024,768]{1,0:T(8,128)(2,1)}, bf16[1024,768]{1,0:T(8,128)(2,1)}, u32[]{:S(2)}, u32[]{:S(2)}) collective-permute-start(bf16[1024,768]{1,0:T(8,128)(2,1)} %pad_maximum_fusion.2.k0.v0), channel_id=1, source_target_pairs={{1,0},{2,1},{3,2},{4,3},{5,4},{6,5},{7,6},{9,8},{10,9},{11,10},{12... | collective-permute-start | bytes 4718600 | tf_op jit(solution)/shard_map/ppermute | solution.py:21
  380.7 50.3 %collective-permute-start.6 = (bf16[1024,512]{1,0:T(8,128)(2,1)}, bf16[1024,512]{1,0:T(8,128)(2,1)}, u32[]{:S(2)}, u32[]{:S(2)}) collective-permute-start(bf16[1024,512]{1,0:T(8,128)(2,1)} %pad_maximum_fusion.3.k0.v0), channel_id=1, source_target_pairs={{0,1},{1,2},{2,3},{3,4},{4,5},{5,6},{6,7},{8,9},{9,10},{10,11},{11... | collective-permute-start | bytes 3145736 | tf_op jit(solution)/shard_map/ppermute | solution.py:21
  386.9 44.1 %collective-permute-start.7 = (bf16[1024,512]{1,0:T(8,128)(2,1)}, bf16[1024,512]{1,0:T(8,128)(2,1)}, u32[]{:S(2)}, u32[]{:S(2)}) collective-permute-start(bf16[1024,512]{1,0:T(8,128)(2,1)} %pad_maximum_fusion.3.k0.v0), channel_id=1, source_target_pairs={{1,0},{2,1},{3,2},{4,3},{5,4},{6,5},{7,6},{9,8},{10,9},{11,10},{12... | collective-permute-start | bytes 3145736 | tf_op jit(solution)/shard_map/ppermute | solution.py:21
  442.5 37.6 %copy-start.5 = (s32[4,5]{1,0:T(4,128)S(1)}, s32[4,5]{1,0:T(4,128)}, u32[]{:S(2)}) copy-start(s32[4,5]{1,0:T(4,128)} %param.7) | copy-start | bytes 244
  442.5 115.9 %all-to-all-start = ((bf16[32,8,6656]{2,1,0:T(8,128)(2,1)}), bf16[32,8,6656]{2,1,0:T(8,128)(2,1)S(1)}, u32[]{:S(2)}, u32[]{:S(2)}) async-start(bf16[32,8,6656]{2,1,0:T(8,128)(2,1)} %bitcast.69), calls=%async_computation | async-start | bytes 6815744 | tf_op jit(solution)/shard_map/all_to_all | solution.py:264
Sparse Core Ops, SparseCore 0:
  15.1 365.5 all-reduce.2

commit v3 on v1

--- a/solution.py
+++ b/solution.py
@@ -12,7 +12,7 @@
 HH = 1664
 TOK = 1024
 SHUF = 256
-HEAD_CHUNKS = ((0, 4), (4, 8), (8, 11), (11, 13))
+HEAD_CHUNKS = ((0, 3), (3, 6), (6, 9), (9, 11), (11, 13))
 
 
 def passed_along(value, axis, steps):

time: 560 us -> 568 us (1.014)
  starting transfers between devices: 80.6 us -> 87.4 us
    ppermute x8 -> x10, starting transfers between devices: 28.2 us -> 33.2 us  [passed_along(): lax.ppermute(value, axis, [(source, source + steps) for source in range(i...]
    ppermute x8 -> x10, waiting for transfers between devices: 230 us -> 226 us  [passed_along(): lax.ppermute(value, axis, [(source, source + steps) for source in range(i...]
    pallas_call x4 -> x5, Pallas kernels: 46.6 us -> 50 us  [attend_near(): pl.pallas_call(near_kernel, grid_spec=pltpu.PrefetchScalarGridSpec(num_sc...]
  transfers between devices with their start and end apart: 10 -> 12, of which waited for: 6 -> 8; matrix products, arithmetic and copies ran while one was open for 14% -> 13% of each run, Pallas kernels for 8% -> 9%
where the time goes in v3:
time: 568 us; the launch traced here: 558 us
  waiting for transfers between devices  297 us (52%)
  starting transfers between devices  87.4 us (15%)
  Pallas kernels  67.1 us (12%)
  local copies, waits for them, and re-layouts  54.8 us (10%)
  other arithmetic  32.4 us (6%)
  between operations  19.5 us (3%)
    ppermute x10, waiting for transfers between devices, passed_along(): lax.ppermute(value, axis, [(source, source + steps) for source in range(i...  226 us
    all_to_all x1, waiting for transfers between devices, body(): lax.all_to_all(arranged, ('dp', 'tile'), split_axis=0, concat_axis=0, til...  64.6 us
    all_to_all x1, starting transfers between devices, body(): lax.all_to_all(arranged, ('dp', 'tile'), split_axis=0, concat_axis=0, til...  54.2 us
    pallas_call x5, Pallas kernels, attend_near(): pl.pallas_call(near_kernel, grid_spec=pltpu.PrefetchScalarGridSpec(num_sc...  50 us
    ppermute x10, starting transfers between devices, passed_along(): lax.ppermute(value, axis, [(source, source + steps) for source in range(i...  33.2 us
    pallas_call x1, Pallas kernels, attend_thumb(): pl.pallas_call(thumb_kernel, grid_spec=pltpu.PrefetchScalarGridSpec(num_s...  17.1 us
  transfers between devices with their start and end apart: 12, of which 8 were waited for; matrix products, arithmetic and copies ran while one was open for 13% of the time, Pallas kernels for 9%

profile of v3, /device:TPU:0, one launch (start us, length us, event | category | flops | bytes accessed | tf_op | source)
XLA Modules:
  0.0 557.8 jit_solution(13958747364137147921)
XLA Ops:
  27.4 77.7 %collective-permute-done.k1.v1 = bf16[1024,768]{1,0:T(8,128)(2,1)S(1)} collective-permute-done((bf16[1024,768]{1,0:T(8,128)(2,1)S(1)}, bf16[1024,768]{1,0:T(8,128)(2,1)S(1)}, u32[]{:S(2)}, u32[]{:S(2)}) %collective-permute-start) | collective-permute-done | bytes 1572896 | tf_op jit(solution)/shard_map/ppermute | solution.py:21
  105.1 5.6 collective-permute-start.2
  118.4 6.6 %reshape_reshape.6 = bf16[16,2,16,2,1664]{4,3,2,1,0:T(2,128)(2,1)S(1)} reshape(bf16[1,1,1024,1664]{3,2,1,0:T(8,128)(2,1)} %param.4) | data formatting | bytes 6815744 | tf_op jit(solution)/shard_map/reshape;reshape | solution.py:123
  129.4 7.3 %reshape_reshape.7 = bf16[8,32,6656]{2,1,0:T(8,128)(2,1)S(1)} reshape(bf16[16,16,2,2,1664]{4,3,2,1,0:T(2,128)(2,1)} %bitcast.69) | data formatting | bytes 6815744 | tf_op jit(solution)/shard_map/reshape;reshape | solution.py:166
  161.7 11.0 %shard_map.46 = (f32[1024,1664]{1,0:T(8,128)}, f32[13,1024,1]{2,1,0:T(8,128)}, f32[13,1024,1]{2,1,0:T(8,128)}) custom-call(s32[3]{0:T(128)} %add_convert_fusion.flags_ref, bf16[1024,384]{1,0:T(8,128)(2,1)} %get-tuple-element.59.q_ref, bf16[1024,768]{1,0:T(8,128)(2,1)} %copy-done.1, ...), custom_call_target="tpu_custom_call", output_to_operand_aliasing={{0}: (8, {}), {1}: (9, {}), {2}: (10, {})} | custom-call | tf_op jit(solution)/shard_map/pallas_call | solution.py:82
  172.7 16.3 %collective-permute-done.2.k1.v1 = bf16[1024,768]{1,0:T(8,128)(2,1)} collective-permute-done((bf16[1024,768]{1,0:T(8,128)(2,1)}, bf16[1024,768]{1,0:T(8,128)(2,1)}, u32[]{:S(2)}, u32[]{:S(2)}) %collective-permute-start.2) | collective-permute-done | bytes 1572896 | tf_op jit(solution)/shard_map/ppermute | solution.py:21
  189.0 5.5 collective-permute-start.4
  199.6 11.1 %shard_map.47 = (f32[1024,1664]{1,0:T(8,128)}, f32[13,1024,1]{2,1,0:T(8,128)}, f32[13,1024,1]{2,1,0:T(8,128)}) custom-call(s32[3]{0:T(128)} %add_convert_fusion.flags_ref, bf16[1024,384]{1,0:T(8,128)(2,1)} %get-tuple-element.58.q_ref, bf16[1024,768]{1,0:T(8,128)(2,1)} %pad_maximum_fusion.1.k0.v0, ...), custom_call_target="tpu_custom_call", output_to_operand_aliasing={{0}: (8, {}), {1}: (9, {}), {2}: (10, {})} | custom-call | tf_op jit(solution)/shard_map/pallas_call | solution.py:82
  210.7 58.9 %collective-permute-done.4.k1.v1 = bf16[1024,768]{1,0:T(8,128)(2,1)} collective-permute-done((bf16[1024,768]{1,0:T(8,128)(2,1)}, bf16[1024,768]{1,0:T(8,128)(2,1)}, u32[]{:S(2)}, u32[]{:S(2)}) %collective-permute-start.4) | collective-permute-done | bytes 1572896 | tf_op jit(solution)/shard_map/ppermute | solution.py:21
  269.6 5.4 collective-permute-start.6
  278.7 11.0 %shard_map.48 = (f32[1024,1664]{1,0:T(8,128)}, f32[13,1024,1]{2,1,0:T(8,128)}, f32[13,1024,1]{2,1,0:T(8,128)}) custom-call(s32[3]{0:T(128)} %add_convert_fusion.flags_ref, bf16[1024,384]{1,0:T(8,128)(2,1)} %get-tuple-element.57.q_ref, bf16[1024,768]{1,0:T(8,128)(2,1)} %pad_maximum_fusion.2.k0.v0, ...), custom_call_target="tpu_custom_call", output_to_operand_aliasing={{0}: (8, {}), {1}: (9, {}), {2}: (10, {})} | custom-call | tf_op jit(solution)/shard_map/pallas_call | solution.py:82
  289.6 34.7 %collective-permute-done.6.k1.v1 = bf16[1024,512]{1,0:T(8,128)(2,1)} collective-permute-done((bf16[1024,512]{1,0:T(8,128)(2,1)}, bf16[1024,512]{1,0:T(8,128)(2,1)}, u32[]{:S(2)}, u32[]{:S(2)}) %collective-permute-start.6) | collective-permute-done | bytes 1048608 | tf_op jit(solution)/shard_map/ppermute | solution.py:21
  324.3 5.3 collective-permute-start.8
  332.0 8.5 %shard_map.49 = (f32[1024,1664]{1,0:T(8,128)}, f32[13,1024,1]{2,1,0:T(8,128)}, f32[13,1024,1]{2,1,0:T(8,128)}) custom-call(s32[3]{0:T(128)} %add_convert_fusion.flags_ref, bf16[1024,256]{1,0:T(8,128)(2,1)} %get-tuple-element.51.q_ref, bf16[1024,512]{1,0:T(8,128)(2,1)} %pad_maximum_fusion.3.k0.v0, ...), custom_call_target="tpu_custom_call", output_to_operand_aliasing={{0}: (8, {}), {1}: (9, {}), {2}: (10, {})} | custom-call | tf_op jit(solution)/shard_map/pallas_call | solution.py:82
  340.4 27.4 %collective-permute-done.8.k1.v1 = bf16[1024,512]{1,0:T(8,128)(2,1)} collective-permute-done((bf16[1024,512]{1,0:T(8,128)(2,1)}, bf16[1024,512]{1,0:T(8,128)(2,1)}, u32[]{:S(2)}, u32[]{:S(2)}) %collective-permute-start.8) | collective-permute-done | bytes 1048608 | tf_op jit(solution)/shard_map/ppermute | solution.py:21
  367.8 10.5 %collective-permute-done.9.k2.v2 = bf16[1024,512]{1,0:T(8,128)(2,1)} collective-permute-done((bf16[1024,512]{1,0:T(8,128)(2,1)}, bf16[1024,512]{1,0:T(8,128)(2,1)}, u32[]{:S(2)}, u32[]{:S(2)}) %collective-permute-start.9) | collective-permute-done | bytes 1048608 | tf_op jit(solution)/shard_map/ppermute | solution.py:21
  378.4 8.5 %shard_map.50 = (f32[1024,1664]{1,0:T(8,128)}, f32[13,1024,1]{2,1,0:T(8,128)}, f32[13,1024,1]{2,1,0:T(8,128)}) custom-call(s32[3]{0:T(128)} %add_convert_fusion.flags_ref, bf16[1024,256]{1,0:T(8,128)(2,1)} %get-tuple-element.52.q_ref, bf16[1024,512]{1,0:T(8,128)(2,1)} %pad_maximum_fusion.4.k0.v0, ...), custom_call_target="tpu_custom_call", output_to_operand_aliasing={{0}: (8, {}), {1}: (9, {}), {2}: (10, {})} | custom-call | tf_op jit(solution)/shard_map/pallas_call | solution.py:82
  386.9 6.6 %all-reduce.3.cloned.1.call-done = (bf16[1024,1664]{1,0:T(8,128)(2,1)}, bf16[1024,1664]{1,0:T(8,128)(2,1)}) async-done(((bf16[1024,1664]{1,0:T(8,128)(2,1)}, bf16[1024,1664]{1,0:T(8,128)(2,1)}), (bf16[1024,1664]{1,0:T(8,128)(2,1)}, bf16[1024,1664]{1,0:T(8,128)(2,1)})) %all-reduce.3.cloned.1.call-update) | async-done | bytes 6815760 | tf_op jit(solution)/shard_map/psum | solution.py:177
  393.5 17.1 %shard_map.51 = bf16[256,6656]{1,0:T(8,128)(2,1)} custom-call(s32[3]{0:T(128)} %add_convert_fusion.flags_ref, bf16[1024,1664]{1,0:T(8,128)(2,1)} %bitcast.67, bf16[1024,1664]{1,0:T(8,128)(2,1)} %get-tuple-element.43.k3, bf16[1024,1664]{1,0:T(8,128)(2,1)} %get-tuple-element.44.v3, f32[1024,1664]{1,0:T(8,128)} %get-tuple-element.40.acc_in, ...), custom_call_target="tpu_custom_call" | custom-call | tf_op jit(solution)/shard_map/pallas_call | solution.py:102
  410.6 54.2 %all-to-all-start = ((bf16[32,8,6656]{2,1,0:T(8,128)(2,1)}), bf16[32,8,6656]{2,1,0:T(8,128)(2,1)S(1)}, u32[]{:S(2)}, u32[]{:S(2)}) async-start(bf16[32,8,6656]{2,1,0:T(8,128)(2,1)} %bitcast.68), calls=%async_computation | async-start | bytes 6815744 | tf_op jit(solution)/shard_map/all_to_all | solution.py:201
  465.5 7.7 %and_or_fusion = (pred[32]{0:T(512)(128)(4,1)S(1)}, s32[32,1]{0,1:T(1,128)S(1)}, s32[32]{0:T(128)S(1)}, pred[32]{0:T(512)(128)(4,1)S(1)}) fusion(s32[]{:T(128)} %bitcast.8, s32[]{:T(128)} %bitcast.7, s32[]{:T(128)} %bitcast.6, s32[]{:T(128)} %bitcast.5, s32[]{:T(128)} %bitcast.3, s32[]{:T(128)} %bitcast.2, s32[]{:T(128)} %bitcast.1, s32[]{:T(128)} %bitcast, ...), kind=kLoop, calls=%fused_computation.32 | loop fusion | flops 1120 | bytes 368 | tf_op jit(solution)/shard_map/or | solution.py:208
  473.2 5.1 and_select_fusion
  478.5 64.6 %all-to-all-done = bf16[32,8,6656]{2,1,0:T(8,128)(2,1)S(1)} async-done(((bf16[32,8,6656]{2,1,0:T(8,128)(2,1)}), bf16[32,8,6656]{2,1,0:T(8,128)(2,1)S(1)}, u32[]{:S(2)}, u32[]{:S(2)}) %all-to-all-start) | async-done | bytes 3407904 | tf_op jit(solution)/shard_map/all_to_all | solution.py:201
  543.1 7.4 %scatter_custom_fusion = bf16[288,6656]{1,0:T(8,128)(2,1)} fusion(s32[256]{0:T(256)S(1)} %bitcast.75, bf16[32,8,6656]{2,1,0:T(8,128)(2,1)S(1)} %all-to-all-done, bf16[]{:T(256)} %constant.98.clone.1), kind=kCustom, calls=%fused_computation.5 | custom fusion | bytes 7241730 | tf_op jit(solution)/shard_map/scatter | solution.py:219
  (53 shorter events, 64.4 us)
Async XLA Ops:
  6.5 387.0 %all-reduce.3.cloned.1.call-start = ((), (), s32[]{:S(2)}) async-start(), calls=%async_computation.1 | async-start | bytes 13631488 | tf_op jit(solution)/shard_map/psum | solution.py:177
  6.5 10.7 %copy-start.4 = (s32[4,5]{1,0:T(4,128)S(1)}, s32[4,5]{1,0:T(4,128)}, u32[]{:S(2)}) copy-start(s32[4,5]{1,0:T(4,128)} %param.7) | copy-start | bytes 244
  11.0 11.7 %copy-start.1 = (bf16[1024,768]{1,0:T(8,128)(2,1)}, bf16[1024,768]{1,0:T(8,128)(2,1)S(1)}, u32[]{:S(2)}) copy-start(bf16[1024,768]{1,0:T(8,128)(2,1)S(1)} %pad_maximum_fusion.k0.v0) | copy-start | bytes 4718596
  11.0 94.2 %collective-permute-start = (bf16[1024,768]{1,0:T(8,128)(2,1)S(1)}, bf16[1024,768]{1,0:T(8,128)(2,1)S(1)}, u32[]{:S(2)}, u32[]{:S(2)}) collective-permute-start(bf16[1024,768]{1,0:T(8,128)(2,1)S(1)} %pad_maximum_fusion.k0.v0), channel_id=1, source_target_pairs={{0,1},{1,2},{2,3},{3,4},{4,5},{5,6},{6,7},{8,9},{9,10},{10,11},{11... | collective-permute-start | bytes 4718600 | tf_op jit(solution)/shard_map/ppermute | solution.py:21
  15.9 89.2 %collective-permute-start.1 = (bf16[1024,768]{1,0:T(8,128)(2,1)S(1)}, bf16[1024,768]{1,0:T(8,128)(2,1)}, u32[]{:S(2)}, u32[]{:S(2)}) collective-permute-start(bf16[1024,768]{1,0:T(8,128)(2,1)S(1)} %pad_maximum_fusion.k0.v0), channel_id=1, source_target_pairs={{1,0},{2,1},{3,2},{4,3},{5,4},{6,5},{7,6},{9,8},{10,9},{11,10},{12... | collective-permute-start | bytes 4718600 | tf_op jit(solution)/shard_map/ppermute | solution.py:21
  18.5 4.1 copy-start.2
  105.1 13.3 %copy-start.3 = (bf16[1024,768]{1,0:T(8,128)(2,1)}, bf16[1024,768]{1,0:T(8,128)(2,1)S(1)}, u32[]{:S(2)}) copy-start(bf16[1024,768]{1,0:T(8,128)(2,1)S(1)} %collective-permute-done.k1.v1) | copy-start | bytes 4718596
  105.1 83.9 %collective-permute-start.2 = (bf16[1024,768]{1,0:T(8,128)(2,1)}, bf16[1024,768]{1,0:T(8,128)(2,1)}, u32[]{:S(2)}, u32[]{:S(2)}) collective-permute-start(bf16[1024,768]{1,0:T(8,128)(2,1)} %pad_maximum_fusion.1.k0.v0), channel_id=1, source_target_pairs={{0,1},{1,2},{2,3},{3,4},{4,5},{5,6},{6,7},{8,9},{9,10},{10,11},{11... | collective-permute-start | bytes 4718600 | tf_op jit(solution)/shard_map/ppermute | solution.py:21
  110.7 78.3 %collective-permute-start.3 = (bf16[1024,768]{1,0:T(8,128)(2,1)}, bf16[1024,768]{1,0:T(8,128)(2,1)}, u32[]{:S(2)}, u32[]{:S(2)}) collective-permute-start(bf16[1024,768]{1,0:T(8,128)(2,1)} %pad_maximum_fusion.1.k0.v0), channel_id=1, source_target_pairs={{1,0},{2,1},{3,2},{4,3},{5,4},{6,5},{7,6},{9,8},{10,9},{11,10},{12... | collective-permute-start | bytes 4718600 | tf_op jit(solution)/shard_map/ppermute | solution.py:21
  145.7 185.2 %copy-start = (bf16[4,256,1664]{2,1,0:T(8,128)(2,1)}, bf16[4,256,1664]{2,1,0:T(8,128)(2,1)S(1)}, u32[]{:S(2)}) copy-start(bf16[4,256,1664]{2,1,0:T(8,128)(2,1)S(1)} %copy.22) | copy-start | bytes 10223620
  189.0 80.5 %collective-permute-start.4 = (bf16[1024,768]{1,0:T(8,128)(2,1)}, bf16[1024,768]{1,0:T(8,128)(2,1)}, u32[]{:S(2)}, u32[]{:S(2)}) collective-permute-start(bf16[1024,768]{1,0:T(8,128)(2,1)} %pad_maximum_fusion.2.k0.v0), channel_id=1, source_target_pairs={{0,1},{1,2},{2,3},{3,4},{4,5},{5,6},{6,7},{8,9},{9,10},{10,11},{11... | collective-permute-start | bytes 4718600 | tf_op jit(solution)/shard_map/ppermute | solution.py:21
  194.6 75.0 %collective-permute-start.5 = (bf16[1024,768]{1,0:T(8,128)(2,1)}, bf16[1024,768]{1,0:T(8,128)(2,1)}, u32[]{:S(2)}, u32[]{:S(2)}) collective-permute-start(bf16[1024,768]{1,0:T(8,128)(2,1)} %pad_maximum_fusion.2.k0.v0), channel_id=1, source_target_pairs={{1,0},{2,1},{3,2},{4,3},{5,4},{6,5},{7,6},{9,8},{10,9},{11,10},{12... | collective-permute-start | bytes 4718600 | tf_op jit(solution)/shard_map/ppermute | solution.py:21
  269.6 54.7 %collective-permute-start.6 = (bf16[1024,512]{1,0:T(8,128)(2,1)}, bf16[1024,512]{1,0:T(8,128)(2,1)}, u32[]{:S(2)}, u32[]{:S(2)}) collective-permute-start(bf16[1024,512]{1,0:T(8,128)(2,1)} %pad_maximum_fusion.3.k0.v0), channel_id=1, source_target_pairs={{0,1},{1,2},{2,3},{3,4},{4,5},{5,6},{6,7},{8,9},{9,10},{10,11},{11... | collective-permute-start | bytes 3145736 | tf_op jit(solution)/shard_map/ppermute | solution.py:21
  275.0 49.3 %collective-permute-start.7 = (bf16[1024,512]{1,0:T(8,128)(2,1)}, bf16[1024,512]{1,0:T(8,128)(2,1)}, u32[]{:S(2)}, u32[]{:S(2)}) collective-permute-start(bf16[1024,512]{1,0:T(8,128)(2,1)} %pad_maximum_fusion.3.k0.v0), channel_id=1, source_target_pairs={{1,0},{2,1},{3,2},{4,3},{5,4},{6,5},{7,6},{9,8},{10,9},{11,10},{12... | collective-permute-start | bytes 3145736 | tf_op jit(solution)/shard_map/ppermute | solution.py:21
  324.3 43.5 %collective-permute-start.8 = (bf16[1024,512]{1,0:T(8,128)(2,1)}, bf16[1024,512]{1,0:T(8,128)(2,1)}, u32[]{:S(2)}, u32[]{:S(2)}) collective-permute-start(bf16[1024,512]{1,0:T(8,128)(2,1)} %pad_maximum_fusion.4.k0.v0), channel_id=1, source_target_pairs={{0,1},{1,2},{2,3},{3,4},{4,5},{5,6},{6,7},{8,9},{9,10},{10,11},{11... | collective-permute-start | bytes 3145736 | tf_op jit(solution)/shard_map/ppermute | solution.py:21
  329.6 48.7 %collective-permute-start.9 = (bf16[1024,512]{1,0:T(8,128)(2,1)}, bf16[1024,512]{1,0:T(8,128)(2,1)}, u32[]{:S(2)}, u32[]{:S(2)}) collective-permute-start(bf16[1024,512]{1,0:T(8,128)(2,1)} %pad_maximum_fusion.4.k0.v0), channel_id=1, source_target_pairs={{1,0},{2,1},{3,2},{4,3},{5,4},{6,5},{7,6},{9,8},{10,9},{11,10},{12... | collective-permute-start | bytes 3145736 | tf_op jit(solution)/shard_map/ppermute | solution.py:21
  410.6 132.5 %all-to-all-start = ((bf16[32,8,6656]{2,1,0:T(8,128)(2,1)}), bf16[32,8,6656]{2,1,0:T(8,128)(2,1)S(1)}, u32[]{:S(2)}, u32[]{:S(2)}) async-start(bf16[32,8,6656]{2,1,0:T(8,128)(2,1)} %bitcast.68), calls=%async_computation | async-start | bytes 6815744 | tf_op jit(solution)/shard_map/all_to_all | solution.py:201
Sparse Core Ops, SparseCore 0:
  24.9 368.5 all-reduce.2
